TPU v7x, 128 devices: a whole 4x4x4 slice. The times are simulated.
128 devices in a mesh: xb: 16 (over y, z), yb: 8 (over x, core).
Axes of the slice: x: 4, y: 4, z: 4, core: 2. Of those that a mesh axis runs over, the one named last changes fastest.
Arguments:
- initial_guess: float32 [128, 512, 256], P('xb', 'yb'), may hold values from -4 to 4
- right_side: float32 [128, 512, 256], P('xb', 'yb'), may hold values from -8 to 8
- coefficient: float32 [128, 512, 256], P('xb', 'yb'), may hold values from 0.3 to 3
Outputs:
- fine_field: float32 [128, 512, 256], P('xb', 'yb')
- middle_field: float32 [64, 256, 128], P('xb', 'yb')
- lower_field: float32 [32, 128, 64], P('xb', 'yb')
- coarse_field: float32 [16, 64, 32], P('xb', 'yb')
All inputs are finite; a program needn't handle non-finite values.
Results may differ from a plain program's by a relative error of at most 0.00002.
Values sent between devices are 32-bit elements; how exact they have to be, the bound alone decides.
No kernel may reach another device: no remote copies, remote signals or barrier semaphores. Data moves between devices by JAX's collectives and lax.ppermute only.
A program may use at most 192 MiB of HBM per device.

v0:
```python
import jax
import jax.numpy as jnp
from jax import lax
from jax.sharding import PartitionSpec as P


COARSE_ITERS = 8


damping_alpha = 0.05
cheb_theta = 1.15
cheb_delta = 0.85
cheb_sigma = cheb_theta / cheb_delta
cheb_first = 1.0 / cheb_sigma
cheb_second = 1.0 / (2.0 * cheb_sigma - cheb_first)
cheb_carry = cheb_second * cheb_first
cheb_resid = 2.0 * cheb_second / cheb_delta
jacobi_weight = 0.8


def exchange(items, axis, dim, forwards=()):
    count = lax.axis_size(axis)
    low = [[] for _ in items]
    high = [[] for _ in items]
    boxes = [box for box, _, _ in forwards]
    reach = max(-(-width // block.shape[dim]) for block, width in items)
    for hop in range(1, reach + 1):
        for sign in (1, -1):
            pieces = []
            owners = []
            for index, (block, width) in enumerate(items):
                size = block.shape[dim]
                rows = min(size, width - (hop - 1) * size)
                if rows <= 0:
                    continue
                begin = size - rows if sign == 1 else 0
                pieces.append(lax.slice_in_dim(block, begin, begin + rows, axis=dim))
                owners.append(index)
            if hop == 1:
                for index, (box, rows_low, rows_high) in enumerate(forwards):
                    rows = rows_low if sign == 1 else rows_high
                    pieces.append(lax.slice_in_dim(box, rows[0], rows[1], axis=dim))
                    owners.append(-1 - index)
            common = [max(p.shape[d] for p in pieces) for d in (1, 2)]
            joined = jnp.concatenate(
                [
                    jnp.pad(p, ((0, 0), (0, common[0] - p.shape[1]), (0, common[1] - p.shape[2])))
                    for p in pieces
                ],
                axis=0,
            )
            if sign == 1:
                pairs = [(i, i + hop) for i in range(count - hop)]
            else:
                pairs = [(i + hop, i) for i in range(count - hop)]
            got = lax.ppermute(joined, axis, pairs)
            offset = 0
            for index, piece in zip(owners, pieces):
                part = got[offset : offset + piece.shape[0], : piece.shape[1], : piece.shape[2]]
                offset += piece.shape[0]
                if index < 0:
                    box = boxes[-1 - index]
                    parts = [part, box] if sign == 1 else [box, part]
                    boxes[-1 - index] = jnp.concatenate(parts, axis=dim)
                elif sign == 1:
                    low[index].insert(0, part)
                else:
                    high[index].append(part)
    extended = [
        jnp.concatenate(low[i] + [block] + high[i], axis=dim)
        for i, (block, width) in enumerate(items)
    ]
    return extended, boxes


def send(pieces, axis, pairs):
    common = [max(p.shape[d] for p in pieces) for d in (1, 2)]
    joined = jnp.concatenate(
        [
            jnp.pad(p, ((0, 0), (0, common[0] - p.shape[1]), (0, common[1] - p.shape[2])))
            for p in pieces
        ],
        axis=0,
    )
    got = lax.ppermute(joined, axis, pairs)
    parts = []
    offset = 0
    for piece in pieces:
        parts.append(got[offset : offset + piece.shape[0], : piece.shape[1], : piece.shape[2]])
        offset += piece.shape[0]
    return parts


def exchange_once(items, extras, forwards=()):
    count_x = lax.axis_size("xb")
    count_y = lax.axis_size("yb")
    boxes = []
    faces = {}
    for sign in (1, -1):
        pairs = [(i, i + 1) for i in range(count_x - 1)]
        if sign == -1:
            pairs = [(j, i) for i, j in pairs]
        pieces = []
        for block, wx, wy in items:
            size = block.shape[0]
            begin = size - wx if sign == 1 else 0
            pieces.append(block[begin : begin + wx])
        for box, rows_low, rows_high in forwards:
            rows = rows_low if sign == 1 else rows_high
            pieces.append(box[rows[0] : rows[1]])
        faces[("x", sign)] = send(pieces, "xb", pairs)
    for sign in (1, -1):
        pairs = [(i, i + 1) for i in range(count_y - 1)]
        if sign == -1:
            pairs = [(j, i) for i, j in pairs]
        pieces = []
        for block, _, wy in list(items) + [(b, 0, w) for b, w in extras]:
            size = block.shape[1]
            begin = size - wy if sign == 1 else 0
            pieces.append(block[:, begin : begin + wy])
        faces[("y", sign)] = send(pieces, "yb", pairs)
    for sx in (1, -1):
        for sy in (1, -1):
            pairs = []
            for a in range(count_x):
                for b in range(count_y):
                    if 0 <= a + sx < count_x and 0 <= b + sy < count_y:
                        pairs.append((a * count_y + b, (a + sx) * count_y + (b + sy)))
            pieces = []
            for block, wx, wy in items:
                bx, by = block.shape[0], block.shape[1]
                x0 = bx - wx if sx == 1 else 0
                y0 = by - wy if sy == 1 else 0
                pieces.append(block[x0 : x0 + wx, y0 : y0 + wy])
            faces[(sx, sy)] = send(pieces, ("xb", "yb"), pairs)
    for index, (block, wx, wy) in enumerate(items):
        low = jnp.concatenate(
            [faces[(1, 1)][index], faces[("x", 1)][index], faces[(1, -1)][index]], axis=1
        )
        middle = jnp.concatenate(
            [faces[("y", 1)][index], block, faces[("y", -1)][index]], axis=1
        )
        high = jnp.concatenate(
            [faces[(-1, 1)][index], faces[("x", -1)][index], faces[(-1, -1)][index]], axis=1
        )
        boxes.append(jnp.concatenate([low, middle, high], axis=0))
    for index, (block, wy) in enumerate(extras):
        index += len(items)
        boxes.append(
            jnp.concatenate([faces[("y", 1)][index], block, faces[("y", -1)][index]], axis=1)
        )
    for index, (box, _, _) in enumerate(forwards):
        index += len(items)
        boxes.append(
            jnp.concatenate([faces[("x", 1)][index], box, faces[("x", -1)][index]], axis=0)
        )
    return boxes


def pad_z(box):
    return jnp.pad(box, ((0, 0), (0, 0), (1, 1)))


def trim(box):
    return box[1:-1, 1:-1, :]


def neighbours(padded):
    return [
        padded[2:, 1:-1, 1:-1],
        padded[:-2, 1:-1, 1:-1],
        padded[1:-1, 2:, 1:-1],
        padded[1:-1, :-2, 1:-1],
        padded[1:-1, 1:-1, 2:],
        padded[1:-1, 1:-1, :-2],
    ]


def face_weights(padded_coef, scale):
    centre = padded_coef[1:-1, 1:-1, 1:-1]
    weights = [0.5 * scale * (centre + other) for other in neighbours(padded_coef)]
    diagonal = damping_alpha + weights[0]
    for other in weights[1:]:
        diagonal = diagonal + other
    return (weights, diagonal)


def apply_operator(padded, field, weights, diagonal):
    result = diagonal * field
    for weight, other in zip(weights, neighbours(padded)):
        result = result - weight * other
    return result


def pair_matrix(count):
    rows = jnp.arange(count // 2)[:, None]
    cols = jnp.arange(count)[None, :] // 2
    return (rows == cols).astype(jnp.float32)


def restrict_field(field):
    sx, sy, sz = field.shape
    halves = field.reshape(sx // 2, 2, sy, sz)
    summed = halves[:, 0] + halves[:, 1]
    summed = jnp.einsum(
        "xyZ,zZ->xyz", summed, pair_matrix(sz), precision=lax.Precision.HIGHEST
    )
    pairs_y = jnp.broadcast_to(pair_matrix(sy), (sx // 2, sy // 2, sy))
    summed = jnp.einsum(
        "xyY,xYz->xyz", pairs_y, summed, precision=lax.Precision.HIGHEST
    )
    return summed * 0.125


def coarse_solve(right_side, coefficient, scale, extend):
    weights, diagonal = face_weights(extend(coefficient), scale)
    field = jnp.zeros_like(right_side)
    for _ in range(COARSE_ITERS):
        field = (
            field
            + jacobi_weight
            * (right_side - apply_operator(extend(field), field, weights, diagonal))
            / diagonal
        )
    leftover = right_side - apply_operator(extend(field), field, weights, diagonal)
    ones_field = jnp.ones_like(right_side)
    image_ones = apply_operator(extend(ones_field), ones_field, weights, diagonal)
    return field + jnp.sum(leftover) / jnp.sum(image_ones)


def extend_all(field):
    return jnp.pad(field, 1)


def box_weights(padded_coef, scale):
    centre = padded_coef[1:-1, 1:-1, 1:-1]
    outside = centre == 0.0
    weights = [
        jnp.where(outside, 0.0, 0.5 * scale * (centre + other))
        for other in neighbours(padded_coef)
    ]
    diagonal = damping_alpha + weights[0]
    for other in weights[1:]:
        diagonal = diagonal + other
    return (weights, diagonal)


def smooth_box(start, right_side, coefficient, scale):
    weights, diagonal = box_weights(pad_z(coefficient), scale)
    if start is None:
        start = jnp.zeros_like(right_side)
        residual = right_side
    else:
        residual = right_side - apply_operator(pad_z(start), trim(start), weights, diagonal)
        start = trim(start)
    first_step = residual / (cheb_theta * diagonal)
    first = start + first_step
    weights = [trim(w) for w in weights]
    diagonal = trim(diagonal)
    right_side = trim(right_side)
    residual = right_side - apply_operator(pad_z(first), trim(first), weights, diagonal)
    second_step = cheb_carry * trim(first_step) + cheb_resid * residual / diagonal
    second = trim(first) + second_step
    weights = [trim(w) for w in weights]
    diagonal = trim(diagonal)
    residual = trim(right_side) - apply_operator(pad_z(second), trim(second), weights, diagonal)
    return (trim(second), residual)


def collect_grid(right_side, coefficient):
    sx, sy, sz = right_side.shape
    count_x = lax.axis_size("xb")
    count_y = lax.axis_size("yb")
    flat = jnp.concatenate([right_side.reshape(1, -1), coefficient.reshape(1, -1)], axis=1)
    both = lax.all_gather(flat, ("xb", "yb"), axis=0, tiled=True)
    size = sx * sy * sz
    return tuple(
        (
            piece.reshape(count_x, count_y, sx, sy, sz)
            .transpose(0, 2, 1, 3, 4)
            .reshape(count_x * sx, count_y * sy, sz)
            for piece in (both[:, :size], both[:, size:])
        )
    )


def own_block(whole, shape):
    start_x = lax.axis_index("xb") * shape[0]
    start_y = lax.axis_index("yb") * shape[1]
    return lax.dynamic_slice(whole, (start_x, start_y, jnp.int32(0)), shape)


def per_device(initial_guess, right_side, coefficient):
    mid_coef = restrict_field(coefficient)
    low_coef = restrict_field(mid_coef)
    low_size = low_coef.shape[0]
    low_first = min(3, low_size)
    assert low_first == 3 or 2 * low_size >= 3
    guess_b, rhs_b, coef_b, mid_coef_b, low_coef_b = exchange_once(
        [(initial_guess, 3, 7), (right_side, 2, 7), (coefficient, 3, 7)],
        [(mid_coef, 3), (low_coef, 3)],
    )
    fine, fine_res = smooth_box(guess_b, rhs_b[:, 1:-1], coef_b, 1.0)
    fine = fine[:, 4:-4]
    mid_rhs = restrict_field(fine_res)
    mid_rhs_b, mid_coef_b, low_coef_b = exchange(
        [(mid_rhs, 2), (mid_coef_b, 3), (low_coef_b, low_first)], "xb", 0
    )[0]
    middle, mid_res = smooth_box(None, mid_rhs_b, mid_coef_b, 0.25)
    low_rhs = restrict_field(mid_res)
    forwards = ()
    if low_first < 3:
        forwards = ((low_coef_b, (2 * low_size - 3, low_size), (2 * low_size, low_size + 3)),)
    boxes = exchange_once([(low_rhs, 2, 2)], (), forwards)
    low_rhs_b = boxes[0]
    if low_first < 3:
        low_coef_b = boxes[1]
    lower, low_res = smooth_box(None, low_rhs_b, low_coef_b, 0.0625)
    coarse_rhs, coarse_coef = collect_grid(restrict_field(low_res), restrict_field(low_coef))
    coarse_whole = coarse_solve(coarse_rhs, coarse_coef, 0.015625, extend_all)
    sx, sy, sz = right_side.shape
    coarse = own_block(coarse_whole, (sx // 8, sy // 8, sz // 8))
    return (fine, middle, lower, coarse)


def solution(mesh):
    placed = (P("xb", "yb", None), P("xb", "yb", None), P("xb", "yb", None))
    return jax.shard_map(
        per_device,
        mesh=mesh,
        in_specs=placed,
        out_specs=(
            P("xb", "yb", None),
            P("xb", "yb", None),
            P("xb", "yb", None),
            P("xb", "yb", None),
        ),
        check_vma=False,
    )
```

profile of v0, /device:TPU:0, one launch (start us, length us, event | category | flops | bytes accessed | tf_op | source)
XLA Modules:
  0.0 143.5 jit_solution(16992047417525427140)
XLA Ops:
  0.7 1.0 slice_dynamic-update-slice_fusion.5
  1.7 1.3 fusion.218
  3.0 0.2 convolution_multiply_fusion.1
  3.3 0.2 fusion.302
  3.5 0.1 convolution_multiply_fusion.3
  3.7 1.3 collective-permute-start.3
  5.1 1.3 collective-permute-start.4
  6.4 6.4 %collective-permute-start = (f32[8,7,256]{2,1,0:T(8,128)S(1)}, f32[8,7,256]{2,1,0:T(8,128)S(1)}, u32[]{:S(2)}, u32[]{:S(2)}) collective-permute-start(f32[8,7,256]{2,1,0:T(8,128)S(1)} %pad_maximum_fusion.17), channel_id=1, source_target_pairs={{0,9},{1,10},{2,11},{3,12},{4,13},{5,14},{6,15},{8,17},{9,18},{10,... | collective-permute-start | bytes 172040 | tf_op jit(solution)/shard_map/ppermute | solution.py:85
  12.8 0.7 collective-permute-start.2
  13.5 0.7 collective-permute-start.5
  14.3 0.1 fusion.321
  14.6 0.1 collective-permute-done
  14.7 1.3 collective-permute-start.7
  16.0 8.0 %collective-permute-start.1 = (f32[8,64,256]{2,1,0:T(8,128)S(1)}, f32[8,64,256]{2,1,0:T(8,128)S(1)}, u32[]{:S(2)}, u32[]{:S(2)}) collective-permute-start(f32[8,64,256]{2,1,0:T(8,128)S(1)} %pad_maximum_fusion.2), channel_id=1, source_target_pairs={{0,8},{8,16},{16,24},{24,32},{32,40},{40,48},{48,56},{56,64},{64,7... | collective-permute-start | bytes 1572872 | tf_op jit(solution)/shard_map/ppermute | solution.py:85
  24.0 1.3 collective-permute-start.6
  25.4 2.0 %collective-permute-done.7 = f32[8,7,256]{2,1,0:T(8,128)S(1)} collective-permute-done((f32[8,7,256]{2,1,0:T(8,128)S(1)}, f32[8,7,256]{2,1,0:T(8,128)S(1)}, u32[]{:S(2)}, u32[]{:S(2)}) %collective-permute-start.7) | collective-permute-done | bytes 57376 | tf_op jit(solution)/shard_map/ppermute | solution.py:85
  27.5 6.6 %collective-permute-done.1 = f32[8,64,256]{2,1,0:T(8,128)S(1)} collective-permute-done((f32[8,64,256]{2,1,0:T(8,128)S(1)}, f32[8,64,256]{2,1,0:T(8,128)S(1)}, u32[]{:S(2)}, u32[]{:S(2)}) %collective-permute-start.1) | collective-permute-done | bytes 524320 | tf_op jit(solution)/shard_map/ppermute | solution.py:85
  34.2 4.7 %collective-permute-done.6 = f32[8,64,256]{2,1,0:T(8,128)S(1)} collective-permute-done((f32[8,64,256]{2,1,0:T(8,128)S(1)}, f32[8,64,256]{2,1,0:T(8,128)S(1)}, u32[]{:S(2)}, u32[]{:S(2)}) %collective-permute-start.6) | collective-permute-done | bytes 524320 | tf_op jit(solution)/shard_map/ppermute | solution.py:85
  38.9 0.1 maximum_maximum_fusion.1
  39.1 1.2 add_add_fusion
  40.3 0.1 maximum_maximum_fusion
  40.5 0.5 slice-done
  41.2 1.4 slice_add_fusion.4
  42.6 1.4 %fusion.31 = f32[10,74,256]{2,1,0:T(8,128)S(1)} fusion(f32[12,76,256]{2,1,0:T(8,128)S(1)} %get-tuple-element.40, f32[12,76,256]{2,1,0:T(8,128)S(1)} %get-tuple-element.38, f32[12,76,256]{2,1,0:T(8,128)S(1)} %get-tuple-element.39, f32[12,76,256]{2,1,0:T(8,128)S(1)} %get-tuple-element.37, f32[12,76,256]{2,1,0:T(8,128)S(1)} %get-tuple-element.36, ...), kind=kLoop, calls=%fused_computation.70 | loop fusion | flops 3599360 | bytes 13209600 | tf_op jit(solution)/shard_map/add | solution.py:263
  44.0 1.0 fusion.40
  45.0 0.3 fusion.214
  45.3 0.3 convolution_multiply_fusion
  45.7 3.5 %collective-permute-start.8 = (f32[7,38,128]{2,1,0:T(8,128)S(1)}, f32[7,38,128]{2,1,0:T(8,128)S(1)}, u32[]{:S(2)}, u32[]{:S(2)}) collective-permute-start(f32[7,38,128]{2,1,0:T(8,128)S(1)} %get-tuple-element.101), channel_id=1, source_target_pairs={{0,8},{8,16},{16,24},{24,32},{32,40},{40,48},{48,56},{56,64},{64,7... | collective-permute-start | bytes 408584 | tf_op jit(solution)/shard_map/ppermute | solution.py:56
  49.2 1.3 collective-permute-start.9
  50.7 0.9 slice.1247
  51.5 1.1 collective-permute-done.8
  52.6 4.2 %collective-permute-done.9 = f32[7,38,128]{2,1,0:T(8,128)S(1)} collective-permute-done((f32[7,38,128]{2,1,0:T(8,128)S(1)}, f32[7,38,128]{2,1,0:T(8,128)S(1)}, u32[]{:S(2)}, u32[]{:S(2)}) %collective-permute-start.9) | collective-permute-done | bytes 136224 | tf_op jit(solution)/shard_map/ppermute | solution.py:56
  56.9 0.2 multiply_divide_fusion
  57.1 0.2 fusion.246
  57.3 0.7 fusion.272
  58.0 0.2 fusion.298
  58.2 0.1 convolution_multiply_fusion.2
  58.4 6.4 %collective-permute-start.11 = (f32[3,22,64]{2,1,0:T(8,128)S(1)}, f32[3,22,64]{2,1,0:T(8,128)S(1)}, u32[]{:S(2)}, u32[]{:S(2)}) collective-permute-start(f32[3,22,64]{2,1,0:T(8,128)S(1)} %get-tuple-element.103), channel_id=1, source_target_pairs={{0,8},{8,16},{16,24},{24,32},{32,40},{40,48},{48,56},{56,64},{64,7... | collective-permute-start | bytes 50696 | tf_op jit(solution)/shard_map/ppermute | solution.py:85
  64.8 3.8 %collective-permute-start.10 = (f32[2,2,64]{2,1,0:T(2,128)S(1)}, f32[2,2,64]{2,1,0:T(2,128)S(1)}, u32[]{:S(2)}, u32[]{:S(2)}) collective-permute-start(f32[2,2,64]{2,1,0:T(2,128)S(1)} %get-tuple-element.105), channel_id=1, source_target_pairs={{0,9},{1,10},{2,11},{3,12},{4,13},{5,14},{6,15},{8,17},{9,18},{10,... | collective-permute-start | bytes 3080 | tf_op jit(solution)/shard_map/ppermute | solution.py:85
  68.6 6.0 %collective-permute-start.13 = (f32[2,2,64]{2,1,0:T(2,128)S(1)}, f32[2,2,64]{2,1,0:T(2,128)S(1)}, u32[]{:S(2)}, u32[]{:S(2)}) collective-permute-start(f32[2,2,64]{2,1,0:T(2,128)S(1)} %get-tuple-element.105), channel_id=1, source_target_pairs={{0,1},{1,2},{2,3},{3,4},{4,5},{5,6},{6,7},{8,9},{9,10},{10,11},{11... | collective-permute-start | bytes 3080 | tf_op jit(solution)/shard_map/ppermute | solution.py:85
  74.6 0.7 collective-permute-start.12
  75.2 1.3 collective-permute-start.14
  76.5 1.3 collective-permute-start.16
  77.9 5.2 %collective-permute-done.16 = f32[3,22,64]{2,1,0:T(8,128)S(1)} collective-permute-done((f32[3,22,64]{2,1,0:T(8,128)S(1)}, f32[3,22,64]{2,1,0:T(8,128)S(1)}, u32[]{:S(2)}, u32[]{:S(2)}) %collective-permute-start.16) | collective-permute-done | bytes 16928 | tf_op jit(solution)/shard_map/ppermute | solution.py:85
  83.1 0.7 collective-permute-start.15
  83.8 1.3 collective-permute-start.17
  85.2 9.2 %collective-permute-done.17 = f32[2,2,64]{2,1,0:T(2,128)S(1)} collective-permute-done((f32[2,2,64]{2,1,0:T(2,128)S(1)}, f32[2,2,64]{2,1,0:T(2,128)S(1)}, u32[]{:S(2)}, u32[]{:S(2)}) %collective-permute-start.17) | collective-permute-done | bytes 1056 | tf_op jit(solution)/shard_map/ppermute | solution.py:85
  94.4 0.1 multiply_divide_fusion.1
  94.7 0.6 fusion.313
  95.3 0.1 fusion.322
  95.4 0.1 convolution_multiply_fusion.5
  95.6 37.9 %all-gather = f32[128,1,512]{2,1,0:T(1,128)S(1)} all-gather(f32[1,1,512]{2,1,0:T(1,128)S(1)} %maximum_bitcast_fusion), channel_id=1, replica_groups=mesh['xb'=16,'yb'=8] {'xb','yb'}, dimensions={0}, use_global_device_ids=true | all-gather | bytes 264192 | tf_op jit(solution)/shard_map/all_gather | solution.py:275
  133.6 0.2 reshape_transpose_reshape.6
  133.8 0.2 reshape_transpose_reshape.7
  134.0 1.0 fusion.192
  135.0 0.7 fusion.68
  135.7 0.7 fusion.84
  136.4 0.7 fusion.100
  137.1 0.7 fusion.116
  137.7 0.7 fusion.132
  138.4 0.7 fusion.148
  139.1 0.7 fusion.164
  139.9 1.6 %fusion.210 = (f32[]{:T(128)}, f32[]{:T(128)}) fusion(f32[16,64,32]{2,1,0:T(8,128)S(1)} %get-tuple-element.7, f32[16,64,32]{2,1,0:T(8,128)S(1)} %broadcast_in_dim.37, f32[16,64,32]{2,1,0:T(8,128)S(1)} %get-tuple-element.8, f32[16,64,32]{2,1,0:T(8,128)S(1)} %get-tuple-element.9, f32[16,64,32]{2,1,0:T(8,128)S(1)} %get-tuple-element.10, ...), kind=kLoop, calls=%fused_computation.319 | loop fusion | flops 1114110 | bytes 1179656 | tf_op jit(solution)/shard_map/reduce_sum | solution.py:228
  142.9 0.6 dynamic-slice_add_fusion
  (105 shorter events, 1.4 us)
Async XLA Ops:
  0.6 3.0 %copy-start.1 = (f32[8,64,256]{2,1,0:T(8,128)S(1)}, f32[8,64,256]{2,1,0:T(8,128)}, u32[]{:S(2)}) copy-start(f32[8,64,256]{2,1,0:T(8,128)} %param.5) | copy-start | bytes 1572868
  0.6 3.0 %copy-start = (f32[8,64,256]{2,1,0:T(8,128)S(1)}, f32[8,64,256]{2,1,0:T(8,128)}, u32[]{:S(2)}) copy-start(f32[8,64,256]{2,1,0:T(8,128)} %param.4) | copy-start | bytes 1572868
  0.7 5.7 %copy-start.2 = (f32[8,64,256]{2,1,0:T(8,128)S(1)}, f32[8,64,256]{2,1,0:T(8,128)}, u32[]{:S(2)}) copy-start(f32[8,64,256]{2,1,0:T(8,128)} %param.3) | copy-start | bytes 1572868
  3.7 23.6 %collective-permute-start.3 = (f32[30,7,256]{2,1,0:T(8,128)S(1)}, f32[30,7,256]{2,1,0:T(8,128)S(1)}, u32[]{:S(2)}, u32[]{:S(2)}) collective-permute-start(f32[30,7,256]{2,1,0:T(8,128)S(1)} %constant_dynamic-update-slice_fusion), channel_id=1, source_target_pairs={{0,1},{1,2},{2,3},{3,4},{4,5},{5,6},{6,7},{8,9},{9,10},{10,11},{11... | collective-permute-start | bytes 645128 | tf_op jit(solution)/shard_map/ppermute | solution.py:85
  5.1 22.3 %collective-permute-start.4 = (f32[30,7,256]{2,1,0:T(8,128)S(1)}, f32[30,7,256]{2,1,0:T(8,128)S(1)}, u32[]{:S(2)}, u32[]{:S(2)}) collective-permute-start(f32[30,7,256]{2,1,0:T(8,128)S(1)} %constant_dynamic-update-slice_fusion.2), channel_id=1, source_target_pairs={{1,0},{2,1},{3,2},{4,3},{5,4},{6,5},{7,6},{9,8},{10,9},{11,10},{12... | collective-permute-start | bytes 645128 | tf_op jit(solution)/shard_map/ppermute | solution.py:85
  6.4 8.3 %collective-permute-start = (f32[8,7,256]{2,1,0:T(8,128)S(1)}, f32[8,7,256]{2,1,0:T(8,128)S(1)}, u32[]{:S(2)}, u32[]{:S(2)}) collective-permute-start(f32[8,7,256]{2,1,0:T(8,128)S(1)} %pad_maximum_fusion.17), channel_id=1, source_target_pairs={{0,9},{1,10},{2,11},{3,12},{4,13},{5,14},{6,15},{8,17},{9,18},{10,... | collective-permute-start | bytes 172040 | tf_op jit(solution)/shard_map/ppermute | solution.py:85
  12.8 3.2 %collective-permute-start.2 = (f32[8,7,256]{2,1,0:T(8,128)S(1)}, f32[8,7,256]{2,1,0:T(8,128)S(1)}, u32[]{:S(2)}, u32[]{:S(2)}) collective-permute-start(f32[8,7,256]{2,1,0:T(8,128)S(1)} %pad_maximum_fusion.18), channel_id=1, source_target_pairs={{1,8},{2,9},{3,10},{4,11},{5,12},{6,13},{7,14},{9,16},{10,17},{11,... | collective-permute-start | bytes 172040 | tf_op jit(solution)/shard_map/ppermute | solution.py:85
  13.5 10.5 %collective-permute-start.5 = (f32[8,7,256]{2,1,0:T(8,128)S(1)}, f32[8,7,256]{2,1,0:T(8,128)S(1)}, u32[]{:S(2)}, u32[]{:S(2)}) collective-permute-start(f32[8,7,256]{2,1,0:T(8,128)S(1)} %pad_maximum_fusion.19), channel_id=1, source_target_pairs={{8,1},{9,2},{10,3},{11,4},{12,5},{13,6},{14,7},{16,9},{17,10},{18,... | collective-permute-start | bytes 172040 | tf_op jit(solution)/shard_map/ppermute | solution.py:85
  14.7 19.5 %copy-start.3 = (f32[8,7,256]{2,1,0:T(8,128)}, f32[8,7,256]{2,1,0:T(8,128)S(1)}, u32[]{:S(2)}) copy-start(f32[8,7,256]{2,1,0:T(8,128)S(1)} %collective-permute-done) | copy-start | bytes 172036
  14.7 12.6 %collective-permute-start.7 = (f32[8,7,256]{2,1,0:T(8,128)S(1)}, f32[8,7,256]{2,1,0:T(8,128)S(1)}, u32[]{:S(2)}, u32[]{:S(2)}) collective-permute-start(f32[8,7,256]{2,1,0:T(8,128)S(1)} %pad_maximum_fusion.20), channel_id=1, source_target_pairs={{9,0},{10,1},{11,2},{12,3},{13,4},{14,5},{15,6},{17,8},{18,9},{19,... | collective-permute-start | bytes 172040 | tf_op jit(solution)/shard_map/ppermute | solution.py:85
  16.0 18.2 %copy-start.4 = (f32[8,7,256]{2,1,0:T(8,128)}, f32[8,7,256]{2,1,0:T(8,128)S(1)}, u32[]{:S(2)}) copy-start(f32[8,7,256]{2,1,0:T(8,128)S(1)} %collective-permute-done.2) | copy-start | bytes 172036
  16.0 18.1 %collective-permute-start.1 = (f32[8,64,256]{2,1,0:T(8,128)S(1)}, f32[8,64,256]{2,1,0:T(8,128)S(1)}, u32[]{:S(2)}, u32[]{:S(2)}) collective-permute-start(f32[8,64,256]{2,1,0:T(8,128)S(1)} %pad_maximum_fusion.2), channel_id=1, source_target_pairs={{0,8},{8,16},{16,24},{24,32},{32,40},{40,48},{48,56},{56,64},{64,7... | collective-permute-start | bytes 1572872 | tf_op jit(solution)/shard_map/ppermute | solution.py:85
  24.0 10.2 %copy-start.5 = (f32[8,7,256]{2,1,0:T(8,128)}, f32[8,7,256]{2,1,0:T(8,128)S(1)}, u32[]{:S(2)}) copy-start(f32[8,7,256]{2,1,0:T(8,128)S(1)} %collective-permute-done.5) | copy-start | bytes 172036
  24.0 14.8 %collective-permute-start.6 = (f32[8,64,256]{2,1,0:T(8,128)S(1)}, f32[8,64,256]{2,1,0:T(8,128)S(1)}, u32[]{:S(2)}, u32[]{:S(2)}) collective-permute-start(f32[8,64,256]{2,1,0:T(8,128)S(1)} %pad_maximum_fusion.3), channel_id=1, source_target_pairs={{8,0},{16,8},{24,16},{32,24},{40,32},{48,40},{56,48},{64,56},{72,6... | collective-permute-start | bytes 1572872 | tf_op jit(solution)/shard_map/ppermute | solution.py:85
  27.4 11.6 %copy-start.6 = (f32[8,7,256]{2,1,0:T(8,128)}, f32[8,7,256]{2,1,0:T(8,128)S(1)}, u32[]{:S(2)}) copy-start(f32[8,7,256]{2,1,0:T(8,128)S(1)} %collective-permute-done.7) | copy-start | bytes 172036
  40.3 0.7 slice-start
  40.3 0.7 slice-start.1
  40.3 0.7 slice-start.2
  40.3 0.8 slice-start.3
  45.7 7.0 %collective-permute-start.8 = (f32[7,38,128]{2,1,0:T(8,128)S(1)}, f32[7,38,128]{2,1,0:T(8,128)S(1)}, u32[]{:S(2)}, u32[]{:S(2)}) collective-permute-start(f32[7,38,128]{2,1,0:T(8,128)S(1)} %get-tuple-element.101), channel_id=1, source_target_pairs={{0,8},{8,16},{16,24},{24,32},{32,40},{40,48},{48,56},{56,64},{64,7... | collective-permute-start | bytes 408584 | tf_op jit(solution)/shard_map/ppermute | solution.py:56
  49.2 7.6 %collective-permute-start.9 = (f32[7,38,128]{2,1,0:T(8,128)S(1)}, f32[7,38,128]{2,1,0:T(8,128)S(1)}, u32[]{:S(2)}, u32[]{:S(2)}) collective-permute-start(f32[7,38,128]{2,1,0:T(8,128)S(1)} %get-tuple-element.102), channel_id=1, source_target_pairs={{8,0},{16,8},{24,16},{32,24},{40,32},{48,40},{56,48},{64,56},{72,6... | collective-permute-start | bytes 408584 | tf_op jit(solution)/shard_map/ppermute | solution.py:56
  58.4 18.2 %collective-permute-start.11 = (f32[3,22,64]{2,1,0:T(8,128)S(1)}, f32[3,22,64]{2,1,0:T(8,128)S(1)}, u32[]{:S(2)}, u32[]{:S(2)}) collective-permute-start(f32[3,22,64]{2,1,0:T(8,128)S(1)} %get-tuple-element.103), channel_id=1, source_target_pairs={{0,8},{8,16},{16,24},{24,32},{32,40},{40,48},{48,56},{56,64},{64,7... | collective-permute-start | bytes 50696 | tf_op jit(solution)/shard_map/ppermute | solution.py:85
  64.8 19.0 %collective-permute-start.10 = (f32[2,2,64]{2,1,0:T(2,128)S(1)}, f32[2,2,64]{2,1,0:T(2,128)S(1)}, u32[]{:S(2)}, u32[]{:S(2)}) collective-permute-start(f32[2,2,64]{2,1,0:T(2,128)S(1)} %get-tuple-element.105), channel_id=1, source_target_pairs={{0,9},{1,10},{2,11},{3,12},{4,13},{5,14},{6,15},{8,17},{9,18},{10,... | collective-permute-start | bytes 3080 | tf_op jit(solution)/shard_map/ppermute | solution.py:85
  68.6 16.6 %collective-permute-start.13 = (f32[2,2,64]{2,1,0:T(2,128)S(1)}, f32[2,2,64]{2,1,0:T(2,128)S(1)}, u32[]{:S(2)}, u32[]{:S(2)}) collective-permute-start(f32[2,2,64]{2,1,0:T(2,128)S(1)} %get-tuple-element.105), channel_id=1, source_target_pairs={{0,1},{1,2},{2,3},{3,4},{4,5},{5,6},{6,7},{8,9},{9,10},{10,11},{11... | collective-permute-start | bytes 3080 | tf_op jit(solution)/shard_map/ppermute | solution.py:85
  74.6 10.6 %collective-permute-start.12 = (f32[2,2,64]{2,1,0:T(2,128)S(1)}, f32[2,2,64]{2,1,0:T(2,128)S(1)}, u32[]{:S(2)}, u32[]{:S(2)}) collective-permute-start(f32[2,2,64]{2,1,0:T(2,128)S(1)} %get-tuple-element.106), channel_id=1, source_target_pairs={{1,8},{2,9},{3,10},{4,11},{5,12},{6,13},{7,14},{9,16},{10,17},{11,... | collective-permute-start | bytes 3080 | tf_op jit(solution)/shard_map/ppermute | solution.py:85
  75.2 10.0 %collective-permute-start.14 = (f32[2,2,64]{2,1,0:T(2,128)S(1)}, f32[2,2,64]{2,1,0:T(2,128)S(1)}, u32[]{:S(2)}, u32[]{:S(2)}) collective-permute-start(f32[2,2,64]{2,1,0:T(2,128)S(1)} %get-tuple-element.106), channel_id=1, source_target_pairs={{1,0},{2,1},{3,2},{4,3},{5,4},{6,5},{7,6},{9,8},{10,9},{11,10},{12... | collective-permute-start | bytes 3080 | tf_op jit(solution)/shard_map/ppermute | solution.py:85
  76.5 6.6 %collective-permute-start.16 = (f32[3,22,64]{2,1,0:T(8,128)S(1)}, f32[3,22,64]{2,1,0:T(8,128)S(1)}, u32[]{:S(2)}, u32[]{:S(2)}) collective-permute-start(f32[3,22,64]{2,1,0:T(8,128)S(1)} %get-tuple-element.104), channel_id=1, source_target_pairs={{8,0},{16,8},{24,16},{32,24},{40,32},{48,40},{56,48},{64,56},{72,6... | collective-permute-start | bytes 50696 | tf_op jit(solution)/shard_map/ppermute | solution.py:85
  83.1 2.1 %collective-permute-start.15 = (f32[2,2,64]{2,1,0:T(2,128)S(1)}, f32[2,2,64]{2,1,0:T(2,128)S(1)}, u32[]{:S(2)}, u32[]{:S(2)}) collective-permute-start(f32[2,2,64]{2,1,0:T(2,128)S(1)} %get-tuple-element.105), channel_id=1, source_target_pairs={{8,1},{9,2},{10,3},{11,4},{12,5},{13,6},{14,7},{16,9},{17,10},{18,... | collective-permute-start | bytes 3080 | tf_op jit(solution)/shard_map/ppermute | solution.py:85
  83.8 10.6 %collective-permute-start.17 = (f32[2,2,64]{2,1,0:T(2,128)S(1)}, f32[2,2,64]{2,1,0:T(2,128)S(1)}, u32[]{:S(2)}, u32[]{:S(2)}) collective-permute-start(f32[2,2,64]{2,1,0:T(2,128)S(1)} %get-tuple-element.106), channel_id=1, source_target_pairs={{9,0},{10,1},{11,2},{12,3},{13,4},{14,5},{15,6},{17,8},{18,9},{19,... | collective-permute-start | bytes 3080 | tf_op jit(solution)/shard_map/ppermute | solution.py:85
where the time goes:
time: 146 us; the launch traced here: 143 us
  starting transfers between devices  47 us (32%)
  blocking collectives  37.9 us (26%)
  waiting for transfers between devices  33.2 us (23%)
  other arithmetic  15.7 us (11%)
  local copies, waits for them, and re-layouts  3.46 us (2%)
  matrix products  3.22 us (2%)
  between operations  2.98 us (2%)
    ppermute x16, starting transfers between devices, send(): got = lax.ppermute(joined, axis, pairs)  42.2 us
    all_gather x1, blocking collectives, collect_grid(): both = lax.all_gather(flat, ('xb', 'yb'), axis=0, tiled=True)  37.9 us
    ppermute x16, waiting for transfers between devices, send(): got = lax.ppermute(joined, axis, pairs)  27.9 us
    ppermute x2, waiting for transfers between devices, exchange(): got = lax.ppermute(joined, axis, pairs)  5.26 us
    ppermute x2, starting transfers between devices, exchange(): got = lax.ppermute(joined, axis, pairs)  4.81 us
    add x7, other arithmetic, coarse_solve(): field + jacobi_weight * (right_side - apply_operator(extend(field), field...  4.78 us
  transfers between devices with their start and end apart: 18, of which 8 were waited for; matrix products, arithmetic and copies ran while one was open for 1% of the time, Pallas kernels for 0%

commit v1 on v0

--- a/solution.py
+++ b/solution.py
@@ -91,7 +91,7 @@
     return parts
 
 
-def exchange_once(items, extras, forwards=()):
+def exchange_once(items, extras):
     count_x = lax.axis_size("xb")
     count_y = lax.axis_size("yb")
     boxes = []
@@ -105,9 +105,6 @@
             size = block.shape[0]
             begin = size - wx if sign == 1 else 0
             pieces.append(block[begin : begin + wx])
-        for box, rows_low, rows_high in forwards:
-            rows = rows_low if sign == 1 else rows_high
-            pieces.append(box[rows[0] : rows[1]])
         faces[("x", sign)] = send(pieces, "xb", pairs)
     for sign in (1, -1):
         pairs = [(i, i + 1) for i in range(count_y - 1)]
@@ -149,11 +146,6 @@
         boxes.append(
             jnp.concatenate([faces[("y", 1)][index], block, faces[("y", -1)][index]], axis=1)
         )
-    for index, (box, _, _) in enumerate(forwards):
-        index += len(items)
-        boxes.append(
-            jnp.concatenate([faces[("x", 1)][index], box, faces[("x", -1)][index]], axis=0)
-        )
     return boxes
 
 
@@ -272,7 +264,9 @@
     count_x = lax.axis_size("xb")
     count_y = lax.axis_size("yb")
     flat = jnp.concatenate([right_side.reshape(1, -1), coefficient.reshape(1, -1)], axis=1)
-    both = lax.all_gather(flat, ("xb", "yb"), axis=0, tiled=True)
+    both = lax.all_to_all(
+        jnp.broadcast_to(flat, (count_x * count_y, flat.shape[1])), ("xb", "yb"), 0, 0, tiled=True
+    )
     size = sx * sy * sz
     return tuple(
         (
@@ -308,14 +302,14 @@
     )[0]
     middle, mid_res = smooth_box(None, mid_rhs_b, mid_coef_b, 0.25)
     low_rhs = restrict_field(mid_res)
+    (low_rhs_b,) = exchange([(low_rhs, 3)], "yb", 1)[0]
     forwards = ()
     if low_first < 3:
         forwards = ((low_coef_b, (2 * low_size - 3, low_size), (2 * low_size, low_size + 3)),)
-    boxes = exchange_once([(low_rhs, 2, 2)], (), forwards)
-    low_rhs_b = boxes[0]
+    (low_rhs_b,), boxes = exchange([(low_rhs_b, 2)], "xb", 0, forwards)
     if low_first < 3:
-        low_coef_b = boxes[1]
-    lower, low_res = smooth_box(None, low_rhs_b, low_coef_b, 0.0625)
+        (low_coef_b,) = boxes
+    lower, low_res = smooth_box(None, low_rhs_b[:, 1:-1], low_coef_b, 0.0625)
     coarse_rhs, coarse_coef = collect_grid(restrict_field(low_res), restrict_field(low_coef))
     coarse_whole = coarse_solve(coarse_rhs, coarse_coef, 0.015625, extend_all)
     sx, sy, sz = right_side.shape

time: 146 us -> 116 us (0.79)
  blocking collectives: 37.9 us -> 0 us
  waiting for transfers between devices: 33.2 us -> 39.6 us
  starting transfers between devices: 47 us -> 48.7 us
    all_gather x1 -> x0, blocking collectives: 37.9 us -> none  [collect_grid(): both = lax.all_gather(flat, ('xb', 'yb'), axis=0, tiled=True)]
    ppermute x16 -> x8, starting transfers between devices: 42.2 us -> 20.7 us  [send(): got = lax.ppermute(joined, axis, pairs)]
    ppermute x16 -> x8, waiting for transfers between devices: 27.9 us -> 13.6 us  [send(): got = lax.ppermute(joined, axis, pairs)]
    all_to_all x0 -> x1, starting transfers between devices: none -> 12.3 us  [collect_grid(): lax.all_to_all(jnp.broadcast_to(flat, (count_x * count_y, flat.shape[1]))...]
    ppermute x2 -> x6, waiting for transfers between devices: 5.26 us -> 16.4 us  [exchange(): got = lax.ppermute(joined, axis, pairs)]
    ppermute x2 -> x6, starting transfers between devices: 4.81 us -> 15.7 us  [exchange(): got = lax.ppermute(joined, axis, pairs)]
    all_to_all x0 -> x1, waiting for transfers between devices: none -> 9.67 us  [collect_grid(): lax.all_to_all(jnp.broadcast_to(flat, (count_x * count_y, flat.shape[1]))...]
  transfers between devices with their start and end apart: 18 -> 15, of which waited for: 8 -> 10; matrix products, arithmetic and copies ran while one was open for 1% -> 1% of each run, Pallas kernels for 0% -> 0%
where the time goes in v1:
time: 116 us; the launch traced here: 114 us
  starting transfers between devices  48.7 us (42%)
  waiting for transfers between devices  39.6 us (34%)
  other arithmetic  15.6 us (13%)
  local copies, waits for them, and re-layouts  4.3 us (4%)
  matrix products  3.23 us (3%)
  between operations  2.75 us (2%)
    ppermute x8, starting transfers between devices, send(): got = lax.ppermute(joined, axis, pairs)  20.7 us
    ppermute x6, waiting for transfers between devices, exchange(): got = lax.ppermute(joined, axis, pairs)  16.4 us
    ppermute x6, starting transfers between devices, exchange(): got = lax.ppermute(joined, axis, pairs)  15.7 us
    ppermute x8, waiting for transfers between devices, send(): got = lax.ppermute(joined, axis, pairs)  13.6 us
    all_to_all x1, starting transfers between devices, collect_grid(): lax.all_to_all(jnp.broadcast_to(flat, (count_x * count_y, flat.shape[1]))...  12.3 us
    all_to_all x1, waiting for transfers between devices, collect_grid(): lax.all_to_all(jnp.broadcast_to(flat, (count_x * count_y, flat.shape[1]))...  9.67 us
    add x7, other arithmetic, coarse_solve(): field + jacobi_weight * (right_side - apply_operator(extend(field), field...  4.78 us
  transfers between devices with their start and end apart: 15, of which 10 were waited for; matrix products, arithmetic and copies ran while one was open for 1% of the time, Pallas kernels for 0%

profile of v1, /device:TPU:0, one launch (start us, length us, event | category | flops | bytes accessed | tf_op | source)
XLA Modules:
  0.0 114.3 jit_solution(6134443762301116662)
XLA Ops:
  0.7 1.0 slice_dynamic-update-slice_fusion.5
  1.7 1.3 %fusion.218 = f32[4,64,128]{2,1,0:T(8,128)S(1)} fusion(f32[4,2,64,256]{3,2,1,0:T(8,128)} %bitcast.91, s32[256]{0:T(256)S(1)} %and_select_fusion.4), kind=kOutput, calls=%fused_computation.335 | convolution fusion | flops 100761600 | bytes 656384 | tf_op jit(solution)/shard_map/xyZ,zZ->xyz/dot_general | solution.py:197
  3.0 0.2 convolution_multiply_fusion.1
  3.3 0.2 fusion.300
  3.5 0.1 convolution_multiply_fusion.3
  3.7 1.3 %collective-permute-start.3 = (f32[30,7,256]{2,1,0:T(8,128)S(1)}, f32[30,7,256]{2,1,0:T(8,128)S(1)}, u32[]{:S(2)}, u32[]{:S(2)}) collective-permute-start(f32[30,7,256]{2,1,0:T(8,128)S(1)} %constant_dynamic-update-slice_fusion), channel_id=1, source_target_pairs={{0,1},{1,2},{2,3},{3,4},{4,5},{5,6},{6,7},{8,9},{9,10},{10,11},{11... | collective-permute-start | bytes 645128 | tf_op jit(solution)/shard_map/ppermute | solution.py:85
  5.1 1.3 %collective-permute-start.4 = (f32[30,7,256]{2,1,0:T(8,128)S(1)}, f32[30,7,256]{2,1,0:T(8,128)S(1)}, u32[]{:S(2)}, u32[]{:S(2)}) collective-permute-start(f32[30,7,256]{2,1,0:T(8,128)S(1)} %constant_dynamic-update-slice_fusion.2), channel_id=1, source_target_pairs={{1,0},{2,1},{3,2},{4,3},{5,4},{6,5},{7,6},{9,8},{10,9},{11,10},{12... | collective-permute-start | bytes 645128 | tf_op jit(solution)/shard_map/ppermute | solution.py:85
  6.4 6.4 %collective-permute-start = (f32[8,7,256]{2,1,0:T(8,128)S(1)}, f32[8,7,256]{2,1,0:T(8,128)S(1)}, u32[]{:S(2)}, u32[]{:S(2)}) collective-permute-start(f32[8,7,256]{2,1,0:T(8,128)S(1)} %pad_maximum_fusion.18), channel_id=1, source_target_pairs={{0,9},{1,10},{2,11},{3,12},{4,13},{5,14},{6,15},{8,17},{9,18},{10,... | collective-permute-start | bytes 172040 | tf_op jit(solution)/shard_map/ppermute | solution.py:85
  12.8 0.7 collective-permute-start.2
  13.5 0.7 collective-permute-start.5
  14.4 0.3 collective-permute-done
  14.7 1.3 %collective-permute-start.7 = (f32[8,7,256]{2,1,0:T(8,128)S(1)}, f32[8,7,256]{2,1,0:T(8,128)S(1)}, u32[]{:S(2)}, u32[]{:S(2)}) collective-permute-start(f32[8,7,256]{2,1,0:T(8,128)S(1)} %pad_maximum_fusion.21), channel_id=1, source_target_pairs={{9,0},{10,1},{11,2},{12,3},{13,4},{14,5},{15,6},{17,8},{18,9},{19,... | collective-permute-start | bytes 172040 | tf_op jit(solution)/shard_map/ppermute | solution.py:85
  16.0 7.8 %collective-permute-start.1 = (f32[8,64,256]{2,1,0:T(8,128)S(1)}, f32[8,64,256]{2,1,0:T(8,128)S(1)}, u32[]{:S(2)}, u32[]{:S(2)}) collective-permute-start(f32[8,64,256]{2,1,0:T(8,128)S(1)} %pad_maximum_fusion.2), channel_id=1, source_target_pairs={{0,8},{8,16},{16,24},{24,32},{32,40},{40,48},{48,56},{56,64},{64,7... | collective-permute-start | bytes 1572872 | tf_op jit(solution)/shard_map/ppermute | solution.py:85
  23.9 1.3 %collective-permute-start.6 = (f32[8,64,256]{2,1,0:T(8,128)S(1)}, f32[8,64,256]{2,1,0:T(8,128)S(1)}, u32[]{:S(2)}, u32[]{:S(2)}) collective-permute-start(f32[8,64,256]{2,1,0:T(8,128)S(1)} %pad_maximum_fusion.3), channel_id=1, source_target_pairs={{8,0},{16,8},{24,16},{32,24},{40,32},{48,40},{56,48},{64,56},{72,6... | collective-permute-start | bytes 1572872 | tf_op jit(solution)/shard_map/ppermute | solution.py:85
  25.2 2.0 %collective-permute-done.7 = f32[8,7,256]{2,1,0:T(8,128)S(1)} collective-permute-done((f32[8,7,256]{2,1,0:T(8,128)S(1)}, f32[8,7,256]{2,1,0:T(8,128)S(1)}, u32[]{:S(2)}, u32[]{:S(2)}) %collective-permute-start.7) | collective-permute-done | bytes 57376 | tf_op jit(solution)/shard_map/ppermute | solution.py:85
  27.4 6.6 %collective-permute-done.1 = f32[8,64,256]{2,1,0:T(8,128)S(1)} collective-permute-done((f32[8,64,256]{2,1,0:T(8,128)S(1)}, f32[8,64,256]{2,1,0:T(8,128)S(1)}, u32[]{:S(2)}, u32[]{:S(2)}) %collective-permute-start.1) | collective-permute-done | bytes 524320 | tf_op jit(solution)/shard_map/ppermute | solution.py:85
  34.1 4.7 %collective-permute-done.6 = f32[8,64,256]{2,1,0:T(8,128)S(1)} collective-permute-done((f32[8,64,256]{2,1,0:T(8,128)S(1)}, f32[8,64,256]{2,1,0:T(8,128)S(1)}, u32[]{:S(2)}, u32[]{:S(2)}) %collective-permute-start.6) | collective-permute-done | bytes 524320 | tf_op jit(solution)/shard_map/ppermute | solution.py:85
  38.8 0.1 maximum_maximum_fusion.1
  38.9 1.2 %add_add_fusion = (f32[12,76,256]{2,1,0:T(8,128)S(1)}, f32[12,76,256]{2,1,0:T(8,128)S(1)}, f32[12,76,256]{2,1,0:T(8,128)S(1)}, f32[12,76,256]{2,1,0:T(8,128)S(1)...) fusion(f32[14,78,256]{2,1,0:T(8,128)S(1)} %maximum_maximum_fusion.1), kind=kLoop, calls=%fused_computation.61 | loop fusion | flops 5836800 | bytes 12599296 | tf_op jit(solution)/shard_map/add | solution.py:236
  40.2 0.1 maximum_maximum_fusion
  40.4 0.5 slice-done
  41.0 1.4 %slice_add_fusion.4 = (f32[12,76,256]{2,1,0:T(8,128)S(1)}, f32[12,76,256]{2,1,0:T(8,128)S(1)}) fusion(f32[14,78,256]{2,1,0:T(8,128)S(1)} %maximum_maximum_fusion, f32[12,76,256]{2,1,0:T(8,128)S(1)} %get-tuple-element.38, f32[12,76,256]{2,1,0:T(8,128)S(1)} %get-tuple-element.39, f32[12,76,256]{2,1,0:T(8,128)S(1)} %get-tuple-element.37, ...), kind=kLoop, calls=%fused_computation.62 | loop fusion | flops 5369856 | bytes 14811136 | tf_op jit(solution)/shard_map/add | solution.py:249
  42.4 1.4 %fusion.31 = f32[10,74,256]{2,1,0:T(8,128)S(1)} fusion(f32[12,76,256]{2,1,0:T(8,128)S(1)} %get-tuple-element.40, f32[12,76,256]{2,1,0:T(8,128)S(1)} %get-tuple-element.38, f32[12,76,256]{2,1,0:T(8,128)S(1)} %get-tuple-element.39, f32[12,76,256]{2,1,0:T(8,128)S(1)} %get-tuple-element.37, f32[12,76,256]{2,1,0:T(8,128)S(1)} %get-tuple-element.36, ...), kind=kLoop, calls=%fused_computation.70 | loop fusion | flops 3599360 | bytes 13209600 | tf_op jit(solution)/shard_map/add | solution.py:255
  43.8 1.0 fusion.40
  44.9 0.3 fusion.214
  45.2 0.3 convolution_multiply_fusion
  45.5 3.5 %collective-permute-start.8 = (f32[7,38,128]{2,1,0:T(8,128)S(1)}, f32[7,38,128]{2,1,0:T(8,128)S(1)}, u32[]{:S(2)}, u32[]{:S(2)}) collective-permute-start(f32[7,38,128]{2,1,0:T(8,128)S(1)} %get-tuple-element.103), channel_id=1, source_target_pairs={{0,8},{8,16},{16,24},{24,32},{32,40},{40,48},{48,56},{56,64},{64,7... | collective-permute-start | bytes 408584 | tf_op jit(solution)/shard_map/ppermute | solution.py:56
  49.0 1.3 %collective-permute-start.9 = (f32[7,38,128]{2,1,0:T(8,128)S(1)}, f32[7,38,128]{2,1,0:T(8,128)S(1)}, u32[]{:S(2)}, u32[]{:S(2)}) collective-permute-start(f32[7,38,128]{2,1,0:T(8,128)S(1)} %get-tuple-element.104), channel_id=1, source_target_pairs={{8,0},{16,8},{24,16},{32,24},{40,32},{48,40},{56,48},{64,56},{72,6... | collective-permute-start | bytes 408584 | tf_op jit(solution)/shard_map/ppermute | solution.py:56
  50.3 0.1 fusion.319
  50.4 2.0 %collective-permute-done.8 = f32[7,38,128]{2,1,0:T(8,128)S(1)} collective-permute-done((f32[7,38,128]{2,1,0:T(8,128)S(1)}, f32[7,38,128]{2,1,0:T(8,128)S(1)}, u32[]{:S(2)}, u32[]{:S(2)}) %collective-permute-start.8) | collective-permute-done | bytes 136224 | tf_op jit(solution)/shard_map/ppermute | solution.py:56
  52.4 4.2 %collective-permute-done.9 = f32[7,38,128]{2,1,0:T(8,128)S(1)} collective-permute-done((f32[7,38,128]{2,1,0:T(8,128)S(1)}, f32[7,38,128]{2,1,0:T(8,128)S(1)}, u32[]{:S(2)}, u32[]{:S(2)}) %collective-permute-start.9) | collective-permute-done | bytes 136224 | tf_op jit(solution)/shard_map/ppermute | solution.py:56
  56.7 0.2 multiply_divide_fusion
  56.9 0.2 fusion.246
  57.1 0.7 fusion.272
  57.8 0.2 fusion.296
  58.0 0.1 convolution_multiply_fusion.2
  58.2 2.6 %collective-permute-start.10 = (f32[2,3,64]{2,1,0:T(4,128)S(1)}, f32[2,3,64]{2,1,0:T(4,128)S(1)}, u32[]{:S(2)}, u32[]{:S(2)}) collective-permute-start(f32[2,3,64]{2,1,0:T(4,128)S(1)} %get-tuple-element.105), channel_id=1, source_target_pairs={{0,1},{1,2},{2,3},{3,4},{4,5},{5,6},{6,7},{8,9},{9,10},{10,11},{11... | collective-permute-start | bytes 4616 | tf_op jit(solution)/shard_map/ppermute | solution.py:56
  60.8 1.3 %collective-permute-start.11 = (f32[2,3,64]{2,1,0:T(4,128)S(1)}, f32[2,3,64]{2,1,0:T(4,128)S(1)}, u32[]{:S(2)}, u32[]{:S(2)}) collective-permute-start(f32[2,3,64]{2,1,0:T(4,128)S(1)} %get-tuple-element.106), channel_id=1, source_target_pairs={{1,0},{2,1},{3,2},{4,3},{5,4},{6,5},{7,6},{9,8},{10,9},{11,10},{12... | collective-permute-start | bytes 4616 | tf_op jit(solution)/shard_map/ppermute | solution.py:56
  62.2 5.7 %collective-permute-done.11 = f32[2,3,64]{2,1,0:T(4,128)S(1)} collective-permute-done((f32[2,3,64]{2,1,0:T(4,128)S(1)}, f32[2,3,64]{2,1,0:T(4,128)S(1)}, u32[]{:S(2)}, u32[]{:S(2)}) %collective-permute-start.11) | collective-permute-done | bytes 1568 | tf_op jit(solution)/shard_map/ppermute | solution.py:56
  67.9 5.7 %collective-permute-start.12 = (f32[3,22,64]{2,1,0:T(8,128)S(1)}, f32[3,22,64]{2,1,0:T(8,128)S(1)}, u32[]{:S(2)}, u32[]{:S(2)}) collective-permute-start(f32[3,22,64]{2,1,0:T(8,128)S(1)} %get-tuple-element.101), channel_id=1, source_target_pairs={{0,8},{8,16},{16,24},{24,32},{32,40},{40,48},{48,56},{56,64},{64,7... | collective-permute-start | bytes 50696 | tf_op jit(solution)/shard_map/ppermute | solution.py:56
  73.6 0.1 convolution_multiply_fusion.4
  73.8 1.3 %collective-permute-start.13 = (f32[3,22,64]{2,1,0:T(8,128)S(1)}, f32[3,22,64]{2,1,0:T(8,128)S(1)}, u32[]{:S(2)}, u32[]{:S(2)}) collective-permute-start(f32[3,22,64]{2,1,0:T(8,128)S(1)} %get-tuple-element.102), channel_id=1, source_target_pairs={{8,0},{16,8},{24,16},{32,24},{40,32},{48,40},{56,48},{64,56},{72,6... | collective-permute-start | bytes 50696 | tf_op jit(solution)/shard_map/ppermute | solution.py:56
  75.1 0.1 collective-permute-done.12
  75.3 4.4 %collective-permute-done.13 = f32[3,22,64]{2,1,0:T(8,128)S(1)} collective-permute-done((f32[3,22,64]{2,1,0:T(8,128)S(1)}, f32[3,22,64]{2,1,0:T(8,128)S(1)}, u32[]{:S(2)}, u32[]{:S(2)}) %collective-permute-start.13) | collective-permute-done | bytes 16928 | tf_op jit(solution)/shard_map/ppermute | solution.py:56
  79.7 0.1 slice_divide_fusion
  79.9 0.6 fusion.311
  80.5 0.1 fusion.320
  80.7 0.1 convolution_multiply_fusion.5
  80.9 0.9 broadcast_in_dim.38
  81.7 12.3 %all-to-all-start = ((f32[128,1,512]{2,1,0:T(1,128)}), f32[128,1,512]{2,1,0:T(1,128)S(1)}, u32[]{:S(2)}, u32[]{:S(2)}) async-start(f32[128,1,512]{2,1,0:T(1,128)} %broadcast_in_dim.38), calls=%async_computation | async-start | bytes 524288 | tf_op jit(solution)/shard_map/all_to_all | solution.py:267
  94.1 0.8 slice.1248
  94.9 9.7 %all-to-all-done = f32[128,1,512]{2,1,0:T(1,128)S(1)} async-done(((f32[128,1,512]{2,1,0:T(1,128)}), f32[128,1,512]{2,1,0:T(1,128)S(1)}, u32[]{:S(2)}, u32[]{:S(2)}) %all-to-all-start) | async-done | bytes 262176 | tf_op jit(solution)/shard_map/all_to_all | solution.py:267
  104.6 0.2 reshape_transpose_reshape.6
  104.8 0.2 reshape_transpose_reshape.7
  105.0 1.0 fusion.192
  106.0 0.7 fusion.68
  106.7 0.7 fusion.84
  107.4 0.7 fusion.100
  108.1 0.7 fusion.116
  108.7 0.7 fusion.132
  109.4 0.7 fusion.148
  110.1 0.7 fusion.164
  110.9 1.5 %fusion.210 = (f32[]{:T(128)}, f32[]{:T(128)}) fusion(f32[16,64,32]{2,1,0:T(8,128)S(1)} %get-tuple-element.7, f32[16,64,32]{2,1,0:T(8,128)S(1)} %broadcast_in_dim.40, f32[16,64,32]{2,1,0:T(8,128)S(1)} %get-tuple-element.8, f32[16,64,32]{2,1,0:T(8,128)S(1)} %get-tuple-element.9, f32[16,64,32]{2,1,0:T(8,128)S(1)} %get-tuple-element.10, ...), kind=kLoop, calls=%fused_computation.319 | loop fusion | flops 1114110 | bytes 1179656 | tf_op jit(solution)/shard_map/reduce_sum | solution.py:220
  113.7 0.6 dynamic-slice_add_fusion
  (99 shorter events, 1.3 us)
Async XLA Ops:
  0.6 3.0 %copy-start.1 = (f32[8,64,256]{2,1,0:T(8,128)S(1)}, f32[8,64,256]{2,1,0:T(8,128)}, u32[]{:S(2)}) copy-start(f32[8,64,256]{2,1,0:T(8,128)} %param.5) | copy-start | bytes 1572868
  0.6 3.0 %copy-start = (f32[8,64,256]{2,1,0:T(8,128)S(1)}, f32[8,64,256]{2,1,0:T(8,128)}, u32[]{:S(2)}) copy-start(f32[8,64,256]{2,1,0:T(8,128)} %param.4) | copy-start | bytes 1572868
  0.7 5.7 %copy-start.2 = (f32[8,64,256]{2,1,0:T(8,128)S(1)}, f32[8,64,256]{2,1,0:T(8,128)}, u32[]{:S(2)}) copy-start(f32[8,64,256]{2,1,0:T(8,128)} %param.3) | copy-start | bytes 1572868
  3.7 23.5 %collective-permute-start.3 = (f32[30,7,256]{2,1,0:T(8,128)S(1)}, f32[30,7,256]{2,1,0:T(8,128)S(1)}, u32[]{:S(2)}, u32[]{:S(2)}) collective-permute-start(f32[30,7,256]{2,1,0:T(8,128)S(1)} %constant_dynamic-update-slice_fusion), channel_id=1, source_target_pairs={{0,1},{1,2},{2,3},{3,4},{4,5},{5,6},{6,7},{8,9},{9,10},{10,11},{11... | collective-permute-start | bytes 645128 | tf_op jit(solution)/shard_map/ppermute | solution.py:85
  5.1 22.2 %collective-permute-start.4 = (f32[30,7,256]{2,1,0:T(8,128)S(1)}, f32[30,7,256]{2,1,0:T(8,128)S(1)}, u32[]{:S(2)}, u32[]{:S(2)}) collective-permute-start(f32[30,7,256]{2,1,0:T(8,128)S(1)} %constant_dynamic-update-slice_fusion.2), channel_id=1, source_target_pairs={{1,0},{2,1},{3,2},{4,3},{5,4},{6,5},{7,6},{9,8},{10,9},{11,10},{12... | collective-permute-start | bytes 645128 | tf_op jit(solution)/shard_map/ppermute | solution.py:85
  6.4 8.3 %collective-permute-start = (f32[8,7,256]{2,1,0:T(8,128)S(1)}, f32[8,7,256]{2,1,0:T(8,128)S(1)}, u32[]{:S(2)}, u32[]{:S(2)}) collective-permute-start(f32[8,7,256]{2,1,0:T(8,128)S(1)} %pad_maximum_fusion.18), channel_id=1, source_target_pairs={{0,9},{1,10},{2,11},{3,12},{4,13},{5,14},{6,15},{8,17},{9,18},{10,... | collective-permute-start | bytes 172040 | tf_op jit(solution)/shard_map/ppermute | solution.py:85
  12.8 3.2 %collective-permute-start.2 = (f32[8,7,256]{2,1,0:T(8,128)S(1)}, f32[8,7,256]{2,1,0:T(8,128)S(1)}, u32[]{:S(2)}, u32[]{:S(2)}) collective-permute-start(f32[8,7,256]{2,1,0:T(8,128)S(1)} %pad_maximum_fusion.19), channel_id=1, source_target_pairs={{1,8},{2,9},{3,10},{4,11},{5,12},{6,13},{7,14},{9,16},{10,17},{11,... | collective-permute-start | bytes 172040 | tf_op jit(solution)/shard_map/ppermute | solution.py:85
  13.5 10.3 %collective-permute-start.5 = (f32[8,7,256]{2,1,0:T(8,128)S(1)}, f32[8,7,256]{2,1,0:T(8,128)S(1)}, u32[]{:S(2)}, u32[]{:S(2)}) collective-permute-start(f32[8,7,256]{2,1,0:T(8,128)S(1)} %pad_maximum_fusion.20), channel_id=1, source_target_pairs={{8,1},{9,2},{10,3},{11,4},{12,5},{13,6},{14,7},{16,9},{17,10},{18,... | collective-permute-start | bytes 172040 | tf_op jit(solution)/shard_map/ppermute | solution.py:85
  14.7 19.3 %copy-start.3 = (f32[8,7,256]{2,1,0:T(8,128)}, f32[8,7,256]{2,1,0:T(8,128)S(1)}, u32[]{:S(2)}) copy-start(f32[8,7,256]{2,1,0:T(8,128)S(1)} %collective-permute-done) | copy-start | bytes 172036
  14.7 12.5 %collective-permute-start.7 = (f32[8,7,256]{2,1,0:T(8,128)S(1)}, f32[8,7,256]{2,1,0:T(8,128)S(1)}, u32[]{:S(2)}, u32[]{:S(2)}) collective-permute-start(f32[8,7,256]{2,1,0:T(8,128)S(1)} %pad_maximum_fusion.21), channel_id=1, source_target_pairs={{9,0},{10,1},{11,2},{12,3},{13,4},{14,5},{15,6},{17,8},{18,9},{19,... | collective-permute-start | bytes 172040 | tf_op jit(solution)/shard_map/ppermute | solution.py:85
  16.0 18.0 %copy-start.4 = (f32[8,7,256]{2,1,0:T(8,128)}, f32[8,7,256]{2,1,0:T(8,128)S(1)}, u32[]{:S(2)}) copy-start(f32[8,7,256]{2,1,0:T(8,128)S(1)} %collective-permute-done.2) | copy-start | bytes 172036
  16.0 18.0 %collective-permute-start.1 = (f32[8,64,256]{2,1,0:T(8,128)S(1)}, f32[8,64,256]{2,1,0:T(8,128)S(1)}, u32[]{:S(2)}, u32[]{:S(2)}) collective-permute-start(f32[8,64,256]{2,1,0:T(8,128)S(1)} %pad_maximum_fusion.2), channel_id=1, source_target_pairs={{0,8},{8,16},{16,24},{24,32},{32,40},{40,48},{48,56},{56,64},{64,7... | collective-permute-start | bytes 1572872 | tf_op jit(solution)/shard_map/ppermute | solution.py:85
  23.9 10.2 %copy-start.5 = (f32[8,7,256]{2,1,0:T(8,128)}, f32[8,7,256]{2,1,0:T(8,128)S(1)}, u32[]{:S(2)}) copy-start(f32[8,7,256]{2,1,0:T(8,128)S(1)} %collective-permute-done.5) | copy-start | bytes 172036
  23.9 14.8 %collective-permute-start.6 = (f32[8,64,256]{2,1,0:T(8,128)S(1)}, f32[8,64,256]{2,1,0:T(8,128)S(1)}, u32[]{:S(2)}, u32[]{:S(2)}) collective-permute-start(f32[8,64,256]{2,1,0:T(8,128)S(1)} %pad_maximum_fusion.3), channel_id=1, source_target_pairs={{8,0},{16,8},{24,16},{32,24},{40,32},{48,40},{56,48},{64,56},{72,6... | collective-permute-start | bytes 1572872 | tf_op jit(solution)/shard_map/ppermute | solution.py:85
  27.2 11.6 %copy-start.6 = (f32[8,7,256]{2,1,0:T(8,128)}, f32[8,7,256]{2,1,0:T(8,128)S(1)}, u32[]{:S(2)}) copy-start(f32[8,7,256]{2,1,0:T(8,128)S(1)} %collective-permute-done.7) | copy-start | bytes 172036
  40.1 0.7 slice-start
  40.2 0.7 slice-start.1
  40.2 0.7 slice-start.2
  40.2 0.7 slice-start.3
  45.5 7.0 %collective-permute-start.8 = (f32[7,38,128]{2,1,0:T(8,128)S(1)}, f32[7,38,128]{2,1,0:T(8,128)S(1)}, u32[]{:S(2)}, u32[]{:S(2)}) collective-permute-start(f32[7,38,128]{2,1,0:T(8,128)S(1)} %get-tuple-element.103), channel_id=1, source_target_pairs={{0,8},{8,16},{16,24},{24,32},{32,40},{40,48},{48,56},{56,64},{64,7... | collective-permute-start | bytes 408584 | tf_op jit(solution)/shard_map/ppermute | solution.py:56
  49.0 7.6 %collective-permute-start.9 = (f32[7,38,128]{2,1,0:T(8,128)S(1)}, f32[7,38,128]{2,1,0:T(8,128)S(1)}, u32[]{:S(2)}, u32[]{:S(2)}) collective-permute-start(f32[7,38,128]{2,1,0:T(8,128)S(1)} %get-tuple-element.104), channel_id=1, source_target_pairs={{8,0},{16,8},{24,16},{32,24},{40,32},{48,40},{56,48},{64,56},{72,6... | collective-permute-start | bytes 408584 | tf_op jit(solution)/shard_map/ppermute | solution.py:56
  58.2 4.0 %collective-permute-start.10 = (f32[2,3,64]{2,1,0:T(4,128)S(1)}, f32[2,3,64]{2,1,0:T(4,128)S(1)}, u32[]{:S(2)}, u32[]{:S(2)}) collective-permute-start(f32[2,3,64]{2,1,0:T(4,128)S(1)} %get-tuple-element.105), channel_id=1, source_target_pairs={{0,1},{1,2},{2,3},{3,4},{4,5},{5,6},{6,7},{8,9},{9,10},{10,11},{11... | collective-permute-start | bytes 4616 | tf_op jit(solution)/shard_map/ppermute | solution.py:56
  60.8 7.0 %collective-permute-start.11 = (f32[2,3,64]{2,1,0:T(4,128)S(1)}, f32[2,3,64]{2,1,0:T(4,128)S(1)}, u32[]{:S(2)}, u32[]{:S(2)}) collective-permute-start(f32[2,3,64]{2,1,0:T(4,128)S(1)} %get-tuple-element.106), channel_id=1, source_target_pairs={{1,0},{2,1},{3,2},{4,3},{5,4},{6,5},{7,6},{9,8},{10,9},{11,10},{12... | collective-permute-start | bytes 4616 | tf_op jit(solution)/shard_map/ppermute | solution.py:56
  67.9 7.3 %collective-permute-start.12 = (f32[3,22,64]{2,1,0:T(8,128)S(1)}, f32[3,22,64]{2,1,0:T(8,128)S(1)}, u32[]{:S(2)}, u32[]{:S(2)}) collective-permute-start(f32[3,22,64]{2,1,0:T(8,128)S(1)} %get-tuple-element.101), channel_id=1, source_target_pairs={{0,8},{8,16},{16,24},{24,32},{32,40},{40,48},{48,56},{56,64},{64,7... | collective-permute-start | bytes 50696 | tf_op jit(solution)/shard_map/ppermute | solution.py:56
  73.8 5.9 %collective-permute-start.13 = (f32[3,22,64]{2,1,0:T(8,128)S(1)}, f32[3,22,64]{2,1,0:T(8,128)S(1)}, u32[]{:S(2)}, u32[]{:S(2)}) collective-permute-start(f32[3,22,64]{2,1,0:T(8,128)S(1)} %get-tuple-element.102), channel_id=1, source_target_pairs={{8,0},{16,8},{24,16},{32,24},{40,32},{48,40},{56,48},{64,56},{72,6... | collective-permute-start | bytes 50696 | tf_op jit(solution)/shard_map/ppermute | solution.py:56
  81.7 22.8 %all-to-all-start = ((f32[128,1,512]{2,1,0:T(1,128)}), f32[128,1,512]{2,1,0:T(1,128)S(1)}, u32[]{:S(2)}, u32[]{:S(2)}) async-start(f32[128,1,512]{2,1,0:T(1,128)} %broadcast_in_dim.38), calls=%async_computation | async-start | bytes 524288 | tf_op jit(solution)/shard_map/all_to_all | solution.py:267

commit v2 on v1

--- a/solution.py
+++ b/solution.py
@@ -259,22 +259,18 @@
     return (trim(second), residual)
 
 
-def collect_grid(right_side, coefficient):
-    sx, sy, sz = right_side.shape
+def collect_grid(block):
+    sx, sy, sz = block.shape
     count_x = lax.axis_size("xb")
     count_y = lax.axis_size("yb")
-    flat = jnp.concatenate([right_side.reshape(1, -1), coefficient.reshape(1, -1)], axis=1)
-    both = lax.all_to_all(
+    flat = block.reshape(1, -1)
+    every = lax.all_to_all(
         jnp.broadcast_to(flat, (count_x * count_y, flat.shape[1])), ("xb", "yb"), 0, 0, tiled=True
     )
-    size = sx * sy * sz
-    return tuple(
-        (
-            piece.reshape(count_x, count_y, sx, sy, sz)
-            .transpose(0, 2, 1, 3, 4)
-            .reshape(count_x * sx, count_y * sy, sz)
-            for piece in (both[:, :size], both[:, size:])
-        )
+    return (
+        every.reshape(count_x, count_y, sx, sy, sz)
+        .transpose(0, 2, 1, 3, 4)
+        .reshape(count_x * sx, count_y * sy, sz)
     )
 
 
@@ -287,6 +283,7 @@
 def per_device(initial_guess, right_side, coefficient):
     mid_coef = restrict_field(coefficient)
     low_coef = restrict_field(mid_coef)
+    coarse_coef = collect_grid(restrict_field(low_coef))
     low_size = low_coef.shape[0]
     low_first = min(3, low_size)
     assert low_first == 3 or 2 * low_size >= 3
@@ -310,7 +307,7 @@
     if low_first < 3:
         (low_coef_b,) = boxes
     lower, low_res = smooth_box(None, low_rhs_b[:, 1:-1], low_coef_b, 0.0625)
-    coarse_rhs, coarse_coef = collect_grid(restrict_field(low_res), restrict_field(low_coef))
+    coarse_rhs = collect_grid(restrict_field(low_res))
     coarse_whole = coarse_solve(coarse_rhs, coarse_coef, 0.015625, extend_all)
     sx, sy, sz = right_side.shape
     coarse = own_block(coarse_whole, (sx // 8, sy // 8, sz // 8))

time: 116 us -> 126 us (1.086)
  starting transfers between devices: 48.7 us -> 57.6 us
    all_to_all x1 -> x2, starting transfers between devices: 12.3 us -> 21.2 us  [collect_grid(): lax.all_to_all(jnp.broadcast_to(flat, (count_x * count_y, flat.shape[1]))...]
    all_to_all x1 -> x2, waiting for transfers between devices: 9.67 us -> 10 us  [collect_grid(): lax.all_to_all(jnp.broadcast_to(flat, (count_x * count_y, flat.shape[1]))...]
  transfers between devices with their start and end apart: 15 -> 16, of which waited for: 10 -> 10; matrix products, arithmetic and copies ran while one was open for 1% -> 3% of each run, Pallas kernels for 0% -> 0%
where the time goes in v2:
time: 126 us; the launch traced here: 125 us
  starting transfers between devices  57.6 us (46%)
  waiting for transfers between devices  40.1 us (32%)
  other arithmetic  16.3 us (13%)
  local copies, waits for them, and re-layouts  4.86 us (4%)
  matrix products  3.23 us (3%)
  between operations  2.84 us (2%)
    all_to_all x2, starting transfers between devices, collect_grid(): lax.all_to_all(jnp.broadcast_to(flat, (count_x * count_y, flat.shape[1]))...  21.2 us
    ppermute x8, starting transfers between devices, send(): got = lax.ppermute(joined, axis, pairs)  20.7 us
    ppermute x6, waiting for transfers between devices, exchange(): got = lax.ppermute(joined, axis, pairs)  16.5 us
    ppermute x6, starting transfers between devices, exchange(): got = lax.ppermute(joined, axis, pairs)  15.7 us
    ppermute x8, waiting for transfers between devices, send(): got = lax.ppermute(joined, axis, pairs)  13.6 us
    all_to_all x2, waiting for transfers between devices, collect_grid(): lax.all_to_all(jnp.broadcast_to(flat, (count_x * count_y, flat.shape[1]))...  10 us
    add x7, other arithmetic, coarse_solve(): field + jacobi_weight * (right_side - apply_operator(extend(field), field...  4.78 us
  transfers between devices with their start and end apart: 16, of which 10 were waited for; matrix products, arithmetic and copies ran while one was open for 3% of the time, Pallas kernels for 0%

profile of v2, /device:TPU:0, one launch (start us, length us, event | category | flops | bytes accessed | tf_op | source)
XLA Modules:
  0.0 124.9 jit_solution(8916015264671310455)
XLA Ops:
  0.7 1.0 slice_dynamic-update-slice_fusion.5
  1.7 1.3 %fusion.218 = f32[4,64,128]{2,1,0:T(8,128)S(1)} fusion(f32[4,2,64,256]{3,2,1,0:T(8,128)} %bitcast.87, s32[256]{0:T(256)S(1)} %and_select_fusion.4), kind=kOutput, calls=%fused_computation.335 | convolution fusion | flops 100761600 | bytes 656384 | tf_op jit(solution)/shard_map/xyZ,zZ->xyz/dot_general | solution.py:197
  3.0 0.2 convolution_multiply_fusion.1
  3.3 0.2 fusion.300
  3.5 0.1 convolution_multiply_fusion.3
  3.7 1.3 %collective-permute-start.3 = (f32[30,7,256]{2,1,0:T(8,128)S(1)}, f32[30,7,256]{2,1,0:T(8,128)S(1)}, u32[]{:S(2)}, u32[]{:S(2)}) collective-permute-start(f32[30,7,256]{2,1,0:T(8,128)S(1)} %constant_dynamic-update-slice_fusion), channel_id=1, source_target_pairs={{0,1},{1,2},{2,3},{3,4},{4,5},{5,6},{6,7},{8,9},{9,10},{10,11},{11... | collective-permute-start | bytes 645128 | tf_op jit(solution)/shard_map/ppermute | solution.py:85
  5.1 1.3 %collective-permute-start.4 = (f32[30,7,256]{2,1,0:T(8,128)S(1)}, f32[30,7,256]{2,1,0:T(8,128)S(1)}, u32[]{:S(2)}, u32[]{:S(2)}) collective-permute-start(f32[30,7,256]{2,1,0:T(8,128)S(1)} %constant_dynamic-update-slice_fusion.2), channel_id=1, source_target_pairs={{1,0},{2,1},{3,2},{4,3},{5,4},{6,5},{7,6},{9,8},{10,9},{11,10},{12... | collective-permute-start | bytes 645128 | tf_op jit(solution)/shard_map/ppermute | solution.py:85
  6.4 6.4 %collective-permute-start = (f32[8,7,256]{2,1,0:T(8,128)S(1)}, f32[8,7,256]{2,1,0:T(8,128)S(1)}, u32[]{:S(2)}, u32[]{:S(2)}) collective-permute-start(f32[8,7,256]{2,1,0:T(8,128)S(1)} %pad_maximum_fusion.18), channel_id=1, source_target_pairs={{0,9},{1,10},{2,11},{3,12},{4,13},{5,14},{6,15},{8,17},{9,18},{10,... | collective-permute-start | bytes 172040 | tf_op jit(solution)/shard_map/ppermute | solution.py:85
  12.8 0.7 collective-permute-start.2
  13.5 0.7 collective-permute-start.5
  14.4 0.3 collective-permute-done
  14.7 1.3 %collective-permute-start.7 = (f32[8,7,256]{2,1,0:T(8,128)S(1)}, f32[8,7,256]{2,1,0:T(8,128)S(1)}, u32[]{:S(2)}, u32[]{:S(2)}) collective-permute-start(f32[8,7,256]{2,1,0:T(8,128)S(1)} %pad_maximum_fusion.21), channel_id=1, source_target_pairs={{9,0},{10,1},{11,2},{12,3},{13,4},{14,5},{15,6},{17,8},{18,9},{19,... | collective-permute-start | bytes 172040 | tf_op jit(solution)/shard_map/ppermute | solution.py:85
  16.0 7.8 %collective-permute-start.1 = (f32[8,64,256]{2,1,0:T(8,128)S(1)}, f32[8,64,256]{2,1,0:T(8,128)S(1)}, u32[]{:S(2)}, u32[]{:S(2)}) collective-permute-start(f32[8,64,256]{2,1,0:T(8,128)S(1)} %pad_maximum_fusion.2), channel_id=1, source_target_pairs={{0,8},{8,16},{16,24},{24,32},{32,40},{40,48},{48,56},{56,64},{64,7... | collective-permute-start | bytes 1572872 | tf_op jit(solution)/shard_map/ppermute | solution.py:85
  23.9 1.3 %collective-permute-start.6 = (f32[8,64,256]{2,1,0:T(8,128)S(1)}, f32[8,64,256]{2,1,0:T(8,128)S(1)}, u32[]{:S(2)}, u32[]{:S(2)}) collective-permute-start(f32[8,64,256]{2,1,0:T(8,128)S(1)} %pad_maximum_fusion.3), channel_id=1, source_target_pairs={{8,0},{16,8},{24,16},{32,24},{40,32},{48,40},{56,48},{64,56},{72,6... | collective-permute-start | bytes 1572872 | tf_op jit(solution)/shard_map/ppermute | solution.py:85
  25.2 2.0 %collective-permute-done.7 = f32[8,7,256]{2,1,0:T(8,128)S(1)} collective-permute-done((f32[8,7,256]{2,1,0:T(8,128)S(1)}, f32[8,7,256]{2,1,0:T(8,128)S(1)}, u32[]{:S(2)}, u32[]{:S(2)}) %collective-permute-start.7) | collective-permute-done | bytes 57376 | tf_op jit(solution)/shard_map/ppermute | solution.py:85
  27.4 6.6 %collective-permute-done.1 = f32[8,64,256]{2,1,0:T(8,128)S(1)} collective-permute-done((f32[8,64,256]{2,1,0:T(8,128)S(1)}, f32[8,64,256]{2,1,0:T(8,128)S(1)}, u32[]{:S(2)}, u32[]{:S(2)}) %collective-permute-start.1) | collective-permute-done | bytes 524320 | tf_op jit(solution)/shard_map/ppermute | solution.py:85
  34.1 4.7 %collective-permute-done.6 = f32[8,64,256]{2,1,0:T(8,128)S(1)} collective-permute-done((f32[8,64,256]{2,1,0:T(8,128)S(1)}, f32[8,64,256]{2,1,0:T(8,128)S(1)}, u32[]{:S(2)}, u32[]{:S(2)}) %collective-permute-start.6) | collective-permute-done | bytes 524320 | tf_op jit(solution)/shard_map/ppermute | solution.py:85
  38.9 1.2 add_add_fusion
  40.2 0.1 maximum_maximum_fusion
  40.4 0.5 slice-done
  41.0 1.4 %slice_add_fusion.4 = (f32[12,76,256]{2,1,0:T(8,128)S(1)}, f32[12,76,256]{2,1,0:T(8,128)S(1)}) fusion(f32[14,78,256]{2,1,0:T(8,128)S(1)} %maximum_maximum_fusion, f32[12,76,256]{2,1,0:T(8,128)S(1)} %get-tuple-element.38, f32[12,76,256]{2,1,0:T(8,128)S(1)} %get-tuple-element.39, f32[12,76,256]{2,1,0:T(8,128)S(1)} %get-tuple-element.37, ...), kind=kLoop, calls=%fused_computation.62 | loop fusion | flops 5369856 | bytes 14811136 | tf_op jit(solution)/shard_map/add | solution.py:249
  42.4 1.4 %fusion.31 = f32[10,74,256]{2,1,0:T(8,128)S(1)} fusion(f32[12,76,256]{2,1,0:T(8,128)S(1)} %get-tuple-element.40, f32[12,76,256]{2,1,0:T(8,128)S(1)} %get-tuple-element.38, f32[12,76,256]{2,1,0:T(8,128)S(1)} %get-tuple-element.39, f32[12,76,256]{2,1,0:T(8,128)S(1)} %get-tuple-element.37, f32[12,76,256]{2,1,0:T(8,128)S(1)} %get-tuple-element.36, ...), kind=kLoop, calls=%fused_computation.70 | loop fusion | flops 3599360 | bytes 13209600 | tf_op jit(solution)/shard_map/add | solution.py:255
  43.8 1.0 fusion.40
  44.9 0.3 fusion.214
  45.2 0.3 convolution_multiply_fusion
  45.5 3.5 %collective-permute-start.8 = (f32[7,38,128]{2,1,0:T(8,128)S(1)}, f32[7,38,128]{2,1,0:T(8,128)S(1)}, u32[]{:S(2)}, u32[]{:S(2)}) collective-permute-start(f32[7,38,128]{2,1,0:T(8,128)S(1)} %get-tuple-element.101), channel_id=1, source_target_pairs={{0,8},{8,16},{16,24},{24,32},{32,40},{40,48},{48,56},{56,64},{64,7... | collective-permute-start | bytes 408584 | tf_op jit(solution)/shard_map/ppermute | solution.py:56
  49.0 1.3 %collective-permute-start.9 = (f32[7,38,128]{2,1,0:T(8,128)S(1)}, f32[7,38,128]{2,1,0:T(8,128)S(1)}, u32[]{:S(2)}, u32[]{:S(2)}) collective-permute-start(f32[7,38,128]{2,1,0:T(8,128)S(1)} %get-tuple-element.102), channel_id=1, source_target_pairs={{8,0},{16,8},{24,16},{32,24},{40,32},{48,40},{56,48},{64,56},{72,6... | collective-permute-start | bytes 408584 | tf_op jit(solution)/shard_map/ppermute | solution.py:56
  50.4 2.0 %collective-permute-done.8 = f32[7,38,128]{2,1,0:T(8,128)S(1)} collective-permute-done((f32[7,38,128]{2,1,0:T(8,128)S(1)}, f32[7,38,128]{2,1,0:T(8,128)S(1)}, u32[]{:S(2)}, u32[]{:S(2)}) %collective-permute-start.8) | collective-permute-done | bytes 136224 | tf_op jit(solution)/shard_map/ppermute | solution.py:56
  52.4 4.2 %collective-permute-done.9 = f32[7,38,128]{2,1,0:T(8,128)S(1)} collective-permute-done((f32[7,38,128]{2,1,0:T(8,128)S(1)}, f32[7,38,128]{2,1,0:T(8,128)S(1)}, u32[]{:S(2)}, u32[]{:S(2)}) %collective-permute-start.9) | collective-permute-done | bytes 136224 | tf_op jit(solution)/shard_map/ppermute | solution.py:56
  56.7 0.2 multiply_divide_fusion
  56.9 0.2 fusion.246
  57.1 0.7 fusion.272
  57.8 0.2 fusion.296
  58.0 0.1 convolution_multiply_fusion.2
  58.2 2.6 %collective-permute-start.10 = (f32[2,3,64]{2,1,0:T(4,128)S(1)}, f32[2,3,64]{2,1,0:T(4,128)S(1)}, u32[]{:S(2)}, u32[]{:S(2)}) collective-permute-start(f32[2,3,64]{2,1,0:T(4,128)S(1)} %get-tuple-element.103), channel_id=1, source_target_pairs={{0,1},{1,2},{2,3},{3,4},{4,5},{5,6},{6,7},{8,9},{9,10},{10,11},{11... | collective-permute-start | bytes 4616 | tf_op jit(solution)/shard_map/ppermute | solution.py:56
  60.8 1.3 %collective-permute-start.11 = (f32[2,3,64]{2,1,0:T(4,128)S(1)}, f32[2,3,64]{2,1,0:T(4,128)S(1)}, u32[]{:S(2)}, u32[]{:S(2)}) collective-permute-start(f32[2,3,64]{2,1,0:T(4,128)S(1)} %get-tuple-element.104), channel_id=1, source_target_pairs={{1,0},{2,1},{3,2},{4,3},{5,4},{6,5},{7,6},{9,8},{10,9},{11,10},{12... | collective-permute-start | bytes 4616 | tf_op jit(solution)/shard_map/ppermute | solution.py:56
  62.2 5.7 %collective-permute-done.11 = f32[2,3,64]{2,1,0:T(4,128)S(1)} collective-permute-done((f32[2,3,64]{2,1,0:T(4,128)S(1)}, f32[2,3,64]{2,1,0:T(4,128)S(1)}, u32[]{:S(2)}, u32[]{:S(2)}) %collective-permute-start.11) | collective-permute-done | bytes 1568 | tf_op jit(solution)/shard_map/ppermute | solution.py:56
  67.9 5.7 %collective-permute-start.12 = (f32[3,22,64]{2,1,0:T(8,128)S(1)}, f32[3,22,64]{2,1,0:T(8,128)S(1)}, u32[]{:S(2)}, u32[]{:S(2)}) collective-permute-start(f32[3,22,64]{2,1,0:T(8,128)S(1)} %get-tuple-element.99), channel_id=1, source_target_pairs={{0,8},{8,16},{16,24},{24,32},{32,40},{40,48},{48,56},{56,64},{64,7... | collective-permute-start | bytes 50696 | tf_op jit(solution)/shard_map/ppermute | solution.py:56
  73.8 0.7 broadcast_in_dim.85
  74.5 11.4 %all-to-all-start.1 = ((f32[128,1,256]{2,1,0:T(1,128)}), f32[128,1,256]{2,1,0:T(1,128)S(1)}, u32[]{:S(2)}, u32[]{:S(2)}) async-start(f32[128,1,256]{2,1,0:T(1,128)} %broadcast_in_dim.85), calls=%async_computation.1 | async-start | bytes 262144 | tf_op jit(solution)/shard_map/all_to_all | solution.py:267
  85.9 1.3 %collective-permute-start.13 = (f32[3,22,64]{2,1,0:T(8,128)S(1)}, f32[3,22,64]{2,1,0:T(8,128)S(1)}, u32[]{:S(2)}, u32[]{:S(2)}) collective-permute-start(f32[3,22,64]{2,1,0:T(8,128)S(1)} %get-tuple-element.100), channel_id=1, source_target_pairs={{8,0},{16,8},{24,16},{32,24},{40,32},{48,40},{56,48},{64,56},{72,6... | collective-permute-start | bytes 50696 | tf_op jit(solution)/shard_map/ppermute | solution.py:56
  87.3 4.6 %collective-permute-done.13 = f32[3,22,64]{2,1,0:T(8,128)S(1)} collective-permute-done((f32[3,22,64]{2,1,0:T(8,128)S(1)}, f32[3,22,64]{2,1,0:T(8,128)S(1)}, u32[]{:S(2)}, u32[]{:S(2)}) %collective-permute-start.13) | collective-permute-done | bytes 16928 | tf_op jit(solution)/shard_map/ppermute | solution.py:56
  92.0 0.1 slice_divide_fusion
  92.2 0.6 fusion.311
  93.0 0.1 convolution_multiply_fusion.5
  93.2 2.1 %all-to-all-done.1 = f32[128,1,256]{2,1,0:T(1,128)S(1)} async-done(((f32[128,1,256]{2,1,0:T(1,128)}), f32[128,1,256]{2,1,0:T(1,128)S(1)}, u32[]{:S(2)}, u32[]{:S(2)}) %all-to-all-start.1) | async-done | bytes 131104 | tf_op jit(solution)/shard_map/all_to_all | solution.py:267
  95.3 0.7 broadcast_in_dim.83
  96.0 9.8 %all-to-all-start = ((f32[128,1,256]{2,1,0:T(1,128)}), f32[128,1,256]{2,1,0:T(1,128)S(1)}, u32[]{:S(2)}, u32[]{:S(2)}) async-start(f32[128,1,256]{2,1,0:T(1,128)} %broadcast_in_dim.83), calls=%async_computation | async-start | bytes 262144 | tf_op jit(solution)/shard_map/all_to_all | solution.py:267
  105.8 0.3 reduce.1
  106.1 0.2 reshape_transpose_reshape.7
  106.3 0.8 slice.1240
  107.1 7.9 %all-to-all-done = f32[128,1,256]{2,1,0:T(1,128)S(1)} async-done(((f32[128,1,256]{2,1,0:T(1,128)}), f32[128,1,256]{2,1,0:T(1,128)S(1)}, u32[]{:S(2)}, u32[]{:S(2)}) %all-to-all-start) | async-done | bytes 131104 | tf_op jit(solution)/shard_map/all_to_all | solution.py:267
  115.0 0.3 reduce
  115.3 0.2 reshape_transpose_reshape.6
  115.5 1.0 fusion.192
  116.5 0.7 fusion.68
  117.2 0.7 fusion.84
  117.9 0.7 fusion.100
  118.6 0.7 fusion.116
  119.3 0.7 fusion.132
  120.0 0.7 fusion.148
  120.7 0.7 fusion.164
  121.4 1.6 %fusion.210 = (f32[]{:T(128)}, f32[]{:T(128)}) fusion(f32[16,64,32]{2,1,0:T(8,128)S(1)} %get-tuple-element.7, f32[16,64,32]{2,1,0:T(8,128)S(1)} %broadcast_in_dim.87, f32[16,64,32]{2,1,0:T(8,128)S(1)} %get-tuple-element.8, f32[16,64,32]{2,1,0:T(8,128)S(1)} %get-tuple-element.9, f32[16,64,32]{2,1,0:T(8,128)S(1)} %get-tuple-element.10, ...), kind=kLoop, calls=%fused_computation.319 | loop fusion | flops 1114110 | bytes 1179656 | tf_op jit(solution)/shard_map/reduce_sum | solution.py:220
  124.3 0.6 dynamic-slice_add_fusion
  (101 shorter events, 1.7 us)
Async XLA Ops:
  0.6 3.0 %copy-start.1 = (f32[8,64,256]{2,1,0:T(8,128)S(1)}, f32[8,64,256]{2,1,0:T(8,128)}, u32[]{:S(2)}) copy-start(f32[8,64,256]{2,1,0:T(8,128)} %param.5) | copy-start | bytes 1572868
  0.6 3.0 %copy-start = (f32[8,64,256]{2,1,0:T(8,128)S(1)}, f32[8,64,256]{2,1,0:T(8,128)}, u32[]{:S(2)}) copy-start(f32[8,64,256]{2,1,0:T(8,128)} %param.4) | copy-start | bytes 1572868
  0.7 5.7 %copy-start.2 = (f32[8,64,256]{2,1,0:T(8,128)S(1)}, f32[8,64,256]{2,1,0:T(8,128)}, u32[]{:S(2)}) copy-start(f32[8,64,256]{2,1,0:T(8,128)} %param.3) | copy-start | bytes 1572868
  3.7 23.5 %collective-permute-start.3 = (f32[30,7,256]{2,1,0:T(8,128)S(1)}, f32[30,7,256]{2,1,0:T(8,128)S(1)}, u32[]{:S(2)}, u32[]{:S(2)}) collective-permute-start(f32[30,7,256]{2,1,0:T(8,128)S(1)} %constant_dynamic-update-slice_fusion), channel_id=1, source_target_pairs={{0,1},{1,2},{2,3},{3,4},{4,5},{5,6},{6,7},{8,9},{9,10},{10,11},{11... | collective-permute-start | bytes 645128 | tf_op jit(solution)/shard_map/ppermute | solution.py:85
  5.1 22.2 %collective-permute-start.4 = (f32[30,7,256]{2,1,0:T(8,128)S(1)}, f32[30,7,256]{2,1,0:T(8,128)S(1)}, u32[]{:S(2)}, u32[]{:S(2)}) collective-permute-start(f32[30,7,256]{2,1,0:T(8,128)S(1)} %constant_dynamic-update-slice_fusion.2), channel_id=1, source_target_pairs={{1,0},{2,1},{3,2},{4,3},{5,4},{6,5},{7,6},{9,8},{10,9},{11,10},{12... | collective-permute-start | bytes 645128 | tf_op jit(solution)/shard_map/ppermute | solution.py:85
  6.4 8.3 %collective-permute-start = (f32[8,7,256]{2,1,0:T(8,128)S(1)}, f32[8,7,256]{2,1,0:T(8,128)S(1)}, u32[]{:S(2)}, u32[]{:S(2)}) collective-permute-start(f32[8,7,256]{2,1,0:T(8,128)S(1)} %pad_maximum_fusion.18), channel_id=1, source_target_pairs={{0,9},{1,10},{2,11},{3,12},{4,13},{5,14},{6,15},{8,17},{9,18},{10,... | collective-permute-start | bytes 172040 | tf_op jit(solution)/shard_map/ppermute | solution.py:85
  12.8 3.2 %collective-permute-start.2 = (f32[8,7,256]{2,1,0:T(8,128)S(1)}, f32[8,7,256]{2,1,0:T(8,128)S(1)}, u32[]{:S(2)}, u32[]{:S(2)}) collective-permute-start(f32[8,7,256]{2,1,0:T(8,128)S(1)} %pad_maximum_fusion.19), channel_id=1, source_target_pairs={{1,8},{2,9},{3,10},{4,11},{5,12},{6,13},{7,14},{9,16},{10,17},{11,... | collective-permute-start | bytes 172040 | tf_op jit(solution)/shard_map/ppermute | solution.py:85
  13.5 10.3 %collective-permute-start.5 = (f32[8,7,256]{2,1,0:T(8,128)S(1)}, f32[8,7,256]{2,1,0:T(8,128)S(1)}, u32[]{:S(2)}, u32[]{:S(2)}) collective-permute-start(f32[8,7,256]{2,1,0:T(8,128)S(1)} %pad_maximum_fusion.20), channel_id=1, source_target_pairs={{8,1},{9,2},{10,3},{11,4},{12,5},{13,6},{14,7},{16,9},{17,10},{18,... | collective-permute-start | bytes 172040 | tf_op jit(solution)/shard_map/ppermute | solution.py:85
  14.7 19.3 %copy-start.3 = (f32[8,7,256]{2,1,0:T(8,128)}, f32[8,7,256]{2,1,0:T(8,128)S(1)}, u32[]{:S(2)}) copy-start(f32[8,7,256]{2,1,0:T(8,128)S(1)} %collective-permute-done) | copy-start | bytes 172036
  14.7 12.5 %collective-permute-start.7 = (f32[8,7,256]{2,1,0:T(8,128)S(1)}, f32[8,7,256]{2,1,0:T(8,128)S(1)}, u32[]{:S(2)}, u32[]{:S(2)}) collective-permute-start(f32[8,7,256]{2,1,0:T(8,128)S(1)} %pad_maximum_fusion.21), channel_id=1, source_target_pairs={{9,0},{10,1},{11,2},{12,3},{13,4},{14,5},{15,6},{17,8},{18,9},{19,... | collective-permute-start | bytes 172040 | tf_op jit(solution)/shard_map/ppermute | solution.py:85
  16.0 18.0 %copy-start.4 = (f32[8,7,256]{2,1,0:T(8,128)}, f32[8,7,256]{2,1,0:T(8,128)S(1)}, u32[]{:S(2)}) copy-start(f32[8,7,256]{2,1,0:T(8,128)S(1)} %collective-permute-done.2) | copy-start | bytes 172036
  16.0 18.0 %collective-permute-start.1 = (f32[8,64,256]{2,1,0:T(8,128)S(1)}, f32[8,64,256]{2,1,0:T(8,128)S(1)}, u32[]{:S(2)}, u32[]{:S(2)}) collective-permute-start(f32[8,64,256]{2,1,0:T(8,128)S(1)} %pad_maximum_fusion.2), channel_id=1, source_target_pairs={{0,8},{8,16},{16,24},{24,32},{32,40},{40,48},{48,56},{56,64},{64,7... | collective-permute-start | bytes 1572872 | tf_op jit(solution)/shard_map/ppermute | solution.py:85
  23.9 10.2 %copy-start.5 = (f32[8,7,256]{2,1,0:T(8,128)}, f32[8,7,256]{2,1,0:T(8,128)S(1)}, u32[]{:S(2)}) copy-start(f32[8,7,256]{2,1,0:T(8,128)S(1)} %collective-permute-done.5) | copy-start | bytes 172036
  23.9 14.8 %collective-permute-start.6 = (f32[8,64,256]{2,1,0:T(8,128)S(1)}, f32[8,64,256]{2,1,0:T(8,128)S(1)}, u32[]{:S(2)}, u32[]{:S(2)}) collective-permute-start(f32[8,64,256]{2,1,0:T(8,128)S(1)} %pad_maximum_fusion.3), channel_id=1, source_target_pairs={{8,0},{16,8},{24,16},{32,24},{40,32},{48,40},{56,48},{64,56},{72,6... | collective-permute-start | bytes 1572872 | tf_op jit(solution)/shard_map/ppermute | solution.py:85
  27.2 11.6 %copy-start.6 = (f32[8,7,256]{2,1,0:T(8,128)}, f32[8,7,256]{2,1,0:T(8,128)S(1)}, u32[]{:S(2)}) copy-start(f32[8,7,256]{2,1,0:T(8,128)S(1)} %collective-permute-done.7) | copy-start | bytes 172036
  40.1 0.7 slice-start
  40.1 0.7 slice-start.1
  40.2 0.7 slice-start.2
  40.2 0.7 slice-start.3
  45.5 7.0 %collective-permute-start.8 = (f32[7,38,128]{2,1,0:T(8,128)S(1)}, f32[7,38,128]{2,1,0:T(8,128)S(1)}, u32[]{:S(2)}, u32[]{:S(2)}) collective-permute-start(f32[7,38,128]{2,1,0:T(8,128)S(1)} %get-tuple-element.101), channel_id=1, source_target_pairs={{0,8},{8,16},{16,24},{24,32},{32,40},{40,48},{48,56},{56,64},{64,7... | collective-permute-start | bytes 408584 | tf_op jit(solution)/shard_map/ppermute | solution.py:56
  49.0 7.6 %collective-permute-start.9 = (f32[7,38,128]{2,1,0:T(8,128)S(1)}, f32[7,38,128]{2,1,0:T(8,128)S(1)}, u32[]{:S(2)}, u32[]{:S(2)}) collective-permute-start(f32[7,38,128]{2,1,0:T(8,128)S(1)} %get-tuple-element.102), channel_id=1, source_target_pairs={{8,0},{16,8},{24,16},{32,24},{40,32},{48,40},{56,48},{64,56},{72,6... | collective-permute-start | bytes 408584 | tf_op jit(solution)/shard_map/ppermute | solution.py:56
  58.2 4.0 %collective-permute-start.10 = (f32[2,3,64]{2,1,0:T(4,128)S(1)}, f32[2,3,64]{2,1,0:T(4,128)S(1)}, u32[]{:S(2)}, u32[]{:S(2)}) collective-permute-start(f32[2,3,64]{2,1,0:T(4,128)S(1)} %get-tuple-element.103), channel_id=1, source_target_pairs={{0,1},{1,2},{2,3},{3,4},{4,5},{5,6},{6,7},{8,9},{9,10},{10,11},{11... | collective-permute-start | bytes 4616 | tf_op jit(solution)/shard_map/ppermute | solution.py:56
  60.8 7.0 %collective-permute-start.11 = (f32[2,3,64]{2,1,0:T(4,128)S(1)}, f32[2,3,64]{2,1,0:T(4,128)S(1)}, u32[]{:S(2)}, u32[]{:S(2)}) collective-permute-start(f32[2,3,64]{2,1,0:T(4,128)S(1)} %get-tuple-element.104), channel_id=1, source_target_pairs={{1,0},{2,1},{3,2},{4,3},{5,4},{6,5},{7,6},{9,8},{10,9},{11,10},{12... | collective-permute-start | bytes 4616 | tf_op jit(solution)/shard_map/ppermute | solution.py:56
  67.9 19.4 %collective-permute-start.12 = (f32[3,22,64]{2,1,0:T(8,128)S(1)}, f32[3,22,64]{2,1,0:T(8,128)S(1)}, u32[]{:S(2)}, u32[]{:S(2)}) collective-permute-start(f32[3,22,64]{2,1,0:T(8,128)S(1)} %get-tuple-element.99), channel_id=1, source_target_pairs={{0,8},{8,16},{16,24},{24,32},{32,40},{40,48},{48,56},{56,64},{64,7... | collective-permute-start | bytes 50696 | tf_op jit(solution)/shard_map/ppermute | solution.py:56
  74.5 20.8 %all-to-all-start.1 = ((f32[128,1,256]{2,1,0:T(1,128)}), f32[128,1,256]{2,1,0:T(1,128)S(1)}, u32[]{:S(2)}, u32[]{:S(2)}) async-start(f32[128,1,256]{2,1,0:T(1,128)} %broadcast_in_dim.85), calls=%async_computation.1 | async-start | bytes 262144 | tf_op jit(solution)/shard_map/all_to_all | solution.py:267
  85.9 6.0 %collective-permute-start.13 = (f32[3,22,64]{2,1,0:T(8,128)S(1)}, f32[3,22,64]{2,1,0:T(8,128)S(1)}, u32[]{:S(2)}, u32[]{:S(2)}) collective-permute-start(f32[3,22,64]{2,1,0:T(8,128)S(1)} %get-tuple-element.100), channel_id=1, source_target_pairs={{8,0},{16,8},{24,16},{32,24},{40,32},{48,40},{56,48},{64,56},{72,6... | collective-permute-start | bytes 50696 | tf_op jit(solution)/shard_map/ppermute | solution.py:56
  96.0 19.0 %all-to-all-start = ((f32[128,1,256]{2,1,0:T(1,128)}), f32[128,1,256]{2,1,0:T(1,128)S(1)}, u32[]{:S(2)}, u32[]{:S(2)}) async-start(f32[128,1,256]{2,1,0:T(1,128)} %broadcast_in_dim.83), calls=%async_computation | async-start | bytes 262144 | tf_op jit(solution)/shard_map/all_to_all | solution.py:267

commit v3 on v1

--- a/solution.py
+++ b/solution.py
@@ -1,6 +1,8 @@
 import jax
 import jax.numpy as jnp
 from jax import lax
+from jax.experimental import pallas as pl
+from jax.experimental.pallas import tpu as pltpu
 from jax.sharding import PartitionSpec as P
 
 
@@ -168,15 +170,6 @@
     ]
 
 
-def face_weights(padded_coef, scale):
-    centre = padded_coef[1:-1, 1:-1, 1:-1]
-    weights = [0.5 * scale * (centre + other) for other in neighbours(padded_coef)]
-    diagonal = damping_alpha + weights[0]
-    for other in weights[1:]:
-        diagonal = diagonal + other
-    return (weights, diagonal)
-
-
 def apply_operator(padded, field, weights, diagonal):
     result = diagonal * field
     for weight, other in zip(weights, neighbours(padded)):
@@ -202,26 +195,6 @@
         "xyY,xYz->xyz", pairs_y, summed, precision=lax.Precision.HIGHEST
     )
     return summed * 0.125
-
-
-def coarse_solve(right_side, coefficient, scale, extend):
-    weights, diagonal = face_weights(extend(coefficient), scale)
-    field = jnp.zeros_like(right_side)
-    for _ in range(COARSE_ITERS):
-        field = (
-            field
-            + jacobi_weight
-            * (right_side - apply_operator(extend(field), field, weights, diagonal))
-            / diagonal
-        )
-    leftover = right_side - apply_operator(extend(field), field, weights, diagonal)
-    ones_field = jnp.ones_like(right_side)
-    image_ones = apply_operator(extend(ones_field), ones_field, weights, diagonal)
-    return field + jnp.sum(leftover) / jnp.sum(image_ones)
-
-
-def extend_all(field):
-    return jnp.pad(field, 1)
 
 
 def box_weights(padded_coef, scale):
@@ -278,10 +251,45 @@
     )
 
 
-def own_block(whole, shape):
-    start_x = lax.axis_index("xb") * shape[0]
-    start_y = lax.axis_index("yb") * shape[1]
-    return lax.dynamic_slice(whole, (start_x, start_y, jnp.int32(0)), shape)
+def coarse_kernel_body(scale, nx, ny, nz, iters):
+    def body(rhs_ref, coef_ref, out_ref):
+        f = rhs_ref[...]
+        k = coef_ref[...]
+        width = ny * nz
+        row = jax.lax.broadcasted_iota(jnp.int32, (nx, width), 0)
+        lane = jax.lax.broadcasted_iota(jnp.int32, (nx, width), 1)
+        zpos = lane % nz
+        masks = [row < nx - 1, row > 0, lane < width - nz, lane >= nz, zpos < nz - 1, zpos > 0]
+        shifts = [(nx - 1, 0), (1, 0), (width - nz, 1), (nz, 1), (width - 1, 1), (1, 1)]
+        def nbs(a):
+            return [jnp.where(m, pltpu.roll(a, s, ax), 0.0) for m, (s, ax) in zip(masks, shifts)]
+        weights = [(0.5 * scale) * (k + other) for other in nbs(k)]
+        diagonal = damping_alpha + weights[0]
+        for other in weights[1:]:
+            diagonal = diagonal + other
+        def apply(v):
+            result = diagonal * v
+            for w, other in zip(weights, nbs(v)):
+                result = result - w * other
+            return result
+        field = jnp.zeros_like(f)
+        for _ in range(iters):
+            field = field + jacobi_weight * (f - apply(field)) / diagonal
+        leftover = f - apply(field)
+        ones = jnp.ones_like(f)
+        image = diagonal * ones
+        for w, m in zip(weights, masks):
+            image = image - w * jnp.where(m, 1.0, 0.0)
+        out_ref[...] = field + jnp.sum(leftover) / jnp.sum(image)
+    return body
+
+
+def coarse_pallas(rhs2d, coef2d, scale, ny, nz, iters):
+    nx, width = rhs2d.shape
+    return pl.pallas_call(
+        coarse_kernel_body(scale, nx, ny, nz, iters),
+        out_shape=jax.ShapeDtypeStruct((nx, width), jnp.float32),
+    )(rhs2d, coef2d)
 
 
 def per_device(initial_guess, right_side, coefficient):
@@ -311,9 +319,17 @@
         (low_coef_b,) = boxes
     lower, low_res = smooth_box(None, low_rhs_b[:, 1:-1], low_coef_b, 0.0625)
     coarse_rhs, coarse_coef = collect_grid(restrict_field(low_res), restrict_field(low_coef))
-    coarse_whole = coarse_solve(coarse_rhs, coarse_coef, 0.015625, extend_all)
+    nx, ny, nz = coarse_rhs.shape
+    coarse_whole = coarse_pallas(
+        coarse_rhs.reshape(nx, ny * nz), coarse_coef.reshape(nx, ny * nz), 0.015625, ny, nz, COARSE_ITERS
+    )
     sx, sy, sz = right_side.shape
-    coarse = own_block(coarse_whole, (sx // 8, sy // 8, sz // 8))
+    sx, sy, sz = sx // 8, sy // 8, sz // 8
+    coarse = lax.dynamic_slice(
+        coarse_whole,
+        (lax.axis_index("xb") * sx, lax.axis_index("yb") * sy * sz),
+        (sx, sy * sz),
+    ).reshape(sx, sy, sz)
     return (fine, middle, lower, coarse)
 
 

time: 116 us -> 118 us (1.017)
  other arithmetic: 15.6 us -> 7.73 us
  starting transfers between devices: 48.7 us -> 52.9 us
  Pallas kernels: 0 us -> 4.01 us
  local copies, waits for them, and re-layouts: 4.3 us -> 7.76 us
  waiting for transfers between devices: 39.6 us -> 40.9 us
  between operations: 2.75 us -> 1.52 us
    add x8 -> x0, other arithmetic: 5.38 us -> none  [the longest x7 4.78 us: coarse_solve(): field + jacobi_weight * (right_side - apply_operator(extend(field), field...]
    pallas_call x0 -> x1, Pallas kernels: none -> 4.01 us  [coarse_pallas(): pl.pallas_call(coarse_kernel_body(scale, nx, ny, nz, iters), out_shape=ja...]
    ppermute x6, waiting for transfers between devices: 16.4 us -> 19.7 us  [exchange(): got = lax.ppermute(joined, axis, pairs)]
    ppermute x8, waiting for transfers between devices: 13.6 us -> 11.4 us  [send(): got = lax.ppermute(joined, axis, pairs)]
    all_to_all x1, starting transfers between devices: 12.3 us -> 14.3 us  [collect_grid(): lax.all_to_all(jnp.broadcast_to(flat, (count_x * count_y, flat.shape[1]))...]
    slice x2, local copies, waits for them, and re-layouts: 0.03 us -> 1.74 us  [exchange_once(): pieces.append(block[x0:x0 + wx, y0:y0 + wy])]
    ppermute x8, starting transfers between devices: 20.7 us -> 22.4 us  [send(): got = lax.ppermute(joined, axis, pairs)]
    reduce_sum x1 -> x0, other arithmetic: 1.55 us -> none  [coarse_solve(): return field + jnp.sum(leftover) / jnp.sum(image_ones)]
  transfers between devices with their start and end apart: 15 -> 15, of which waited for: 10 -> 8; matrix products, arithmetic and copies ran while one was open for 1% -> 3% of each run, Pallas kernels for 0% -> 0%
where the time goes in v3:
time: 118 us; the launch traced here: 117 us
  starting transfers between devices  52.9 us (45%)
  waiting for transfers between devices  40.9 us (35%)
  local copies, waits for them, and re-layouts  7.76 us (7%)
  other arithmetic  7.73 us (7%)
  Pallas kernels  4.01 us (3%)
  matrix products  2.19 us (2%)
  between operations  1.52 us (1%)
    ppermute x8, starting transfers between devices, send(): got = lax.ppermute(joined, axis, pairs)  22.4 us
    ppermute x6, waiting for transfers between devices, exchange(): got = lax.ppermute(joined, axis, pairs)  19.7 us
    ppermute x6, starting transfers between devices, exchange(): got = lax.ppermute(joined, axis, pairs)  16.2 us
    all_to_all x1, starting transfers between devices, collect_grid(): lax.all_to_all(jnp.broadcast_to(flat, (count_x * count_y, flat.shape[1]))...  14.3 us
    ppermute x8, waiting for transfers between devices, send(): got = lax.ppermute(joined, axis, pairs)  11.4 us
    all_to_all x1, waiting for transfers between devices, collect_grid(): lax.all_to_all(jnp.broadcast_to(flat, (count_x * count_y, flat.shape[1]))...  9.85 us
    pallas_call x1, Pallas kernels, coarse_pallas(): pl.pallas_call(coarse_kernel_body(scale, nx, ny, nz, iters), out_shape=ja...  4.01 us
  transfers between devices with their start and end apart: 15, of which 8 were waited for; matrix products, arithmetic and copies ran while one was open for 3% of the time, Pallas kernels for 0%

profile of v3, /device:TPU:0, one launch (start us, length us, event | category | flops | bytes accessed | tf_op | source)
XLA Modules:
  0.0 117.1 jit_solution(18233232169121642524)
XLA Ops:
  0.7 0.9 fusion.191
  1.5 0.9 fusion.190
  2.4 1.3 %collective-permute-start.7 = (f32[8,7,256]{2,1,0:T(8,128)S(1)}, f32[8,7,256]{2,1,0:T(8,128)S(1)}, u32[]{:S(2)}, u32[]{:S(2)}) collective-permute-start(f32[8,7,256]{2,1,0:T(8,128)S(1)} %pad_maximum_fusion.21), channel_id=1, source_target_pairs={{9,0},{10,1},{11,2},{12,3},{13,4},{14,5},{15,6},{17,8},{18,9},{19,... | collective-permute-start | bytes 172040 | tf_op jit(solution)/shard_map/ppermute | solution.py:87
  3.7 0.7 collective-permute-start.2
  4.4 0.7 collective-permute-start.5
  5.1 9.5 %collective-permute-start = (f32[8,7,256]{2,1,0:T(8,128)S(1)}, f32[8,7,256]{2,1,0:T(8,128)S(1)}, u32[]{:S(2)}, u32[]{:S(2)}) collective-permute-start(f32[8,7,256]{2,1,0:T(8,128)S(1)} %pad_maximum_fusion.18), channel_id=1, source_target_pairs={{0,9},{1,10},{2,11},{3,12},{4,13},{5,14},{6,15},{8,17},{9,18},{10,... | collective-permute-start | bytes 172040 | tf_op jit(solution)/shard_map/ppermute | solution.py:87
  14.7 0.9 slice_dynamic-update-slice_fusion.5
  15.6 0.3 fusion.51
  15.9 0.2 convolution_multiply_fusion.1
  16.2 0.2 fusion.133
  16.3 0.1 convolution_multiply_fusion.3
  16.6 1.3 %collective-permute-start.4 = (f32[30,7,256]{2,1,0:T(8,128)S(1)}, f32[30,7,256]{2,1,0:T(8,128)S(1)}, u32[]{:S(2)}, u32[]{:S(2)}) collective-permute-start(f32[30,7,256]{2,1,0:T(8,128)S(1)} %constant_dynamic-update-slice_fusion.2), channel_id=1, source_target_pairs={{1,0},{2,1},{3,2},{4,3},{5,4},{6,5},{7,6},{9,8},{10,9},{11,10},{12... | collective-permute-start | bytes 645128 | tf_op jit(solution)/shard_map/ppermute | solution.py:87
  17.9 0.1 fusion.193
  18.1 0.0 copy-start.3
  18.1 3.0 %collective-permute-start.3 = (f32[30,7,256]{2,1,0:T(8,128)S(1)}, f32[30,7,256]{2,1,0:T(8,128)S(1)}, u32[]{:S(2)}, u32[]{:S(2)}) collective-permute-start(f32[30,7,256]{2,1,0:T(8,128)S(1)} %constant_dynamic-update-slice_fusion), channel_id=1, source_target_pairs={{0,1},{1,2},{2,3},{3,4},{4,5},{5,6},{6,7},{8,9},{9,10},{10,11},{11... | collective-permute-start | bytes 645128 | tf_op jit(solution)/shard_map/ppermute | solution.py:87
  21.2 1.3 %collective-permute-start.6 = (f32[8,64,256]{2,1,0:T(8,128)S(1)}, f32[8,64,256]{2,1,0:T(8,128)S(1)}, u32[]{:S(2)}, u32[]{:S(2)}) collective-permute-start(f32[8,64,256]{2,1,0:T(8,128)S(1)} %pad_maximum_fusion.3), channel_id=1, source_target_pairs={{8,0},{16,8},{24,16},{32,24},{40,32},{48,40},{56,48},{64,56},{72,6... | collective-permute-start | bytes 1572872 | tf_op jit(solution)/shard_map/ppermute | solution.py:87
  22.6 0.0 copy-start.5
  22.6 4.6 %collective-permute-start.1 = (f32[8,64,256]{2,1,0:T(8,128)S(1)}, f32[8,64,256]{2,1,0:T(8,128)S(1)}, u32[]{:S(2)}, u32[]{:S(2)}) collective-permute-start(f32[8,64,256]{2,1,0:T(8,128)S(1)} %pad_maximum_fusion.2), channel_id=1, source_target_pairs={{0,8},{8,16},{16,24},{24,32},{32,40},{40,48},{48,56},{56,64},{64,7... | collective-permute-start | bytes 1572872 | tf_op jit(solution)/shard_map/ppermute | solution.py:87
  27.4 9.7 %collective-permute-done.6 = f32[8,64,256]{2,1,0:T(8,128)S(1)} collective-permute-done((f32[8,64,256]{2,1,0:T(8,128)S(1)}, f32[8,64,256]{2,1,0:T(8,128)S(1)}, u32[]{:S(2)}, u32[]{:S(2)}) %collective-permute-start.6) | collective-permute-done | bytes 524320 | tf_op jit(solution)/shard_map/ppermute | solution.py:87
  37.1 1.7 %collective-permute-done.1 = f32[8,64,256]{2,1,0:T(8,128)S(1)} collective-permute-done((f32[8,64,256]{2,1,0:T(8,128)S(1)}, f32[8,64,256]{2,1,0:T(8,128)S(1)}, u32[]{:S(2)}, u32[]{:S(2)}) %collective-permute-start.1) | collective-permute-done | bytes 524320 | tf_op jit(solution)/shard_map/ppermute | solution.py:87
  38.9 0.1 maximum_maximum_fusion.1
  39.0 0.0 slice-start
  39.1 1.2 %add_add_fusion = (f32[12,76,256]{2,1,0:T(8,128)S(1)}, f32[12,76,256]{2,1,0:T(8,128)S(1)}, f32[12,76,256]{2,1,0:T(8,128)S(1)}, f32[12,76,256]{2,1,0:T(8,128)S(1)...) fusion(f32[14,78,256]{2,1,0:T(8,128)S(1)} %maximum_maximum_fusion.1), kind=kLoop, calls=%fused_computation.49 | loop fusion | flops 5836800 | bytes 12599296 | tf_op jit(solution)/shard_map/add | solution.py:209
  40.4 0.1 maximum_maximum_fusion.2
  40.5 0.1 maximum_maximum_fusion
  40.6 1.4 %slice_add_fusion.4 = (f32[12,76,256]{2,1,0:T(8,128)S(1)}, f32[12,76,256]{2,1,0:T(8,128)S(1)}) fusion(f32[14,78,256]{2,1,0:T(8,128)S(1)} %maximum_maximum_fusion, f32[12,76,256]{2,1,0:T(8,128)S(1)} %get-tuple-element.29, f32[12,76,256]{2,1,0:T(8,128)S(1)} %get-tuple-element.30, f32[12,76,256]{2,1,0:T(8,128)S(1)} %get-tuple-element.28, ...), kind=kLoop, calls=%fused_computation.50 | loop fusion | flops 5369856 | bytes 14811136 | tf_op jit(solution)/shard_map/add | solution.py:222
  42.0 1.5 %fusion.31 = f32[10,74,256]{2,1,0:T(8,128)S(1)} fusion(f32[12,76,256]{2,1,0:T(8,128)S(1)} %get-tuple-element.31, f32[12,76,256]{2,1,0:T(8,128)S(1)} %get-tuple-element.29, f32[12,76,256]{2,1,0:T(8,128)S(1)} %get-tuple-element.30, f32[12,76,256]{2,1,0:T(8,128)S(1)} %get-tuple-element.28, f32[12,76,256]{2,1,0:T(8,128)S(1)} %get-tuple-element.27, ...), kind=kLoop, calls=%fused_computation.58 | loop fusion | flops 3599360 | bytes 13209600 | tf_op jit(solution)/shard_map/add | solution.py:228
  43.4 1.1 fusion.40
  44.5 0.3 fusion.47
  44.8 0.3 convolution_multiply_fusion
  45.1 5.3 %collective-permute-start.8 = (f32[7,38,128]{2,1,0:T(8,128)S(1)}, f32[7,38,128]{2,1,0:T(8,128)S(1)}, u32[]{:S(2)}, u32[]{:S(2)}) collective-permute-start(f32[7,38,128]{2,1,0:T(8,128)S(1)} %get-tuple-element.94), channel_id=1, source_target_pairs={{0,8},{8,16},{16,24},{24,32},{32,40},{40,48},{48,56},{56,64},{64,7... | collective-permute-start | bytes 408584 | tf_op jit(solution)/shard_map/ppermute | solution.py:58
  50.4 1.3 %collective-permute-start.9 = (f32[7,38,128]{2,1,0:T(8,128)S(1)}, f32[7,38,128]{2,1,0:T(8,128)S(1)}, u32[]{:S(2)}, u32[]{:S(2)}) collective-permute-start(f32[7,38,128]{2,1,0:T(8,128)S(1)} %get-tuple-element.95), channel_id=1, source_target_pairs={{8,0},{16,8},{24,16},{32,24},{40,32},{48,40},{56,48},{64,56},{72,6... | collective-permute-start | bytes 408584 | tf_op jit(solution)/shard_map/ppermute | solution.py:58
  51.7 0.1 fusion.153
  51.8 2.6 %collective-permute-done.8 = f32[7,38,128]{2,1,0:T(8,128)S(1)} collective-permute-done((f32[7,38,128]{2,1,0:T(8,128)S(1)}, f32[7,38,128]{2,1,0:T(8,128)S(1)}, u32[]{:S(2)}, u32[]{:S(2)}) %collective-permute-start.8) | collective-permute-done | bytes 136224 | tf_op jit(solution)/shard_map/ppermute | solution.py:58
  54.5 6.7 %collective-permute-done.9 = f32[7,38,128]{2,1,0:T(8,128)S(1)} collective-permute-done((f32[7,38,128]{2,1,0:T(8,128)S(1)}, f32[7,38,128]{2,1,0:T(8,128)S(1)}, u32[]{:S(2)}, u32[]{:S(2)}) %collective-permute-start.9) | collective-permute-done | bytes 136224 | tf_op jit(solution)/shard_map/ppermute | solution.py:58
  61.2 0.2 multiply_divide_fusion
  61.4 0.2 fusion.80
  61.6 0.7 fusion.106
  62.3 0.2 fusion.129
  62.5 0.1 convolution_multiply_fusion.2
  62.7 1.4 %collective-permute-start.10 = (f32[2,3,64]{2,1,0:T(4,128)S(1)}, f32[2,3,64]{2,1,0:T(4,128)S(1)}, u32[]{:S(2)}, u32[]{:S(2)}) collective-permute-start(f32[2,3,64]{2,1,0:T(4,128)S(1)} %get-tuple-element.96), channel_id=1, source_target_pairs={{0,1},{1,2},{2,3},{3,4},{4,5},{5,6},{6,7},{8,9},{9,10},{10,11},{11... | collective-permute-start | bytes 4616 | tf_op jit(solution)/shard_map/ppermute | solution.py:58
  64.1 1.3 %collective-permute-start.11 = (f32[2,3,64]{2,1,0:T(4,128)S(1)}, f32[2,3,64]{2,1,0:T(4,128)S(1)}, u32[]{:S(2)}, u32[]{:S(2)}) collective-permute-start(f32[2,3,64]{2,1,0:T(4,128)S(1)} %get-tuple-element.97), channel_id=1, source_target_pairs={{1,0},{2,1},{3,2},{4,3},{5,4},{6,5},{7,6},{9,8},{10,9},{11,10},{12... | collective-permute-start | bytes 4616 | tf_op jit(solution)/shard_map/ppermute | solution.py:58
  65.4 3.3 %collective-permute-done.11 = f32[2,3,64]{2,1,0:T(4,128)S(1)} collective-permute-done((f32[2,3,64]{2,1,0:T(4,128)S(1)}, f32[2,3,64]{2,1,0:T(4,128)S(1)}, u32[]{:S(2)}, u32[]{:S(2)}) %collective-permute-start.11) | collective-permute-done | bytes 1568 | tf_op jit(solution)/shard_map/ppermute | solution.py:58
  68.7 5.7 %collective-permute-start.12 = (f32[3,22,64]{2,1,0:T(8,128)S(1)}, f32[3,22,64]{2,1,0:T(8,128)S(1)}, u32[]{:S(2)}, u32[]{:S(2)}) collective-permute-start(f32[3,22,64]{2,1,0:T(8,128)S(1)} %get-tuple-element.92), channel_id=1, source_target_pairs={{0,8},{8,16},{16,24},{24,32},{32,40},{40,48},{48,56},{56,64},{64,7... | collective-permute-start | bytes 50696 | tf_op jit(solution)/shard_map/ppermute | solution.py:58
  74.4 0.1 convolution_multiply_fusion.4
  74.5 0.1 reshape.347
  74.6 1.3 %collective-permute-start.13 = (f32[3,22,64]{2,1,0:T(8,128)S(1)}, f32[3,22,64]{2,1,0:T(8,128)S(1)}, u32[]{:S(2)}, u32[]{:S(2)}) collective-permute-start(f32[3,22,64]{2,1,0:T(8,128)S(1)} %get-tuple-element.93), channel_id=1, source_target_pairs={{8,0},{16,8},{24,16},{32,24},{40,32},{48,40},{56,48},{64,56},{72,6... | collective-permute-start | bytes 50696 | tf_op jit(solution)/shard_map/ppermute | solution.py:58
  75.9 0.1 collective-permute-done.12
  76.1 7.0 %collective-permute-done.13 = f32[3,22,64]{2,1,0:T(8,128)S(1)} collective-permute-done((f32[3,22,64]{2,1,0:T(8,128)S(1)}, f32[3,22,64]{2,1,0:T(8,128)S(1)}, u32[]{:S(2)}, u32[]{:S(2)}) %collective-permute-start.13) | collective-permute-done | bytes 16928 | tf_op jit(solution)/shard_map/ppermute | solution.py:58
  83.1 0.1 slice_divide_fusion
  83.2 0.1 fusion.121
  83.3 0.6 fusion.145
  83.9 0.1 fusion.154
  84.1 0.1 convolution_multiply_fusion.5
  84.2 0.1 reshape.345
  84.3 0.9 broadcast_in_dim.34
  85.2 14.3 %all-to-all-start = ((f32[128,1,512]{2,1,0:T(1,128)}), f32[128,1,512]{2,1,0:T(1,128)S(1)}, u32[]{:S(2)}, u32[]{:S(2)}) async-start(f32[128,1,512]{2,1,0:T(1,128)} %broadcast_in_dim.34), calls=%async_computation | async-start | bytes 524288 | tf_op jit(solution)/shard_map/all_to_all | solution.py:240
  99.5 0.8 slice.983
  100.3 9.8 %all-to-all-done = f32[128,1,512]{2,1,0:T(1,128)S(1)} async-done(((f32[128,1,512]{2,1,0:T(1,128)}), f32[128,1,512]{2,1,0:T(1,128)S(1)}, u32[]{:S(2)}, u32[]{:S(2)}) %all-to-all-start) | async-done | bytes 262176 | tf_op jit(solution)/shard_map/all_to_all | solution.py:240
  110.2 0.7 reshape_reshape_transpose_reshape.7.coef_ref
  110.9 0.7 reshape_reshape_transpose_reshape.6.rhs_ref
  111.6 4.0 %shard_map.66 = f32[16,2048]{1,0:T(8,128)} custom-call(f32[16,2048]{1,0:T(8,128)} %reshape_reshape_transpose_reshape.6.rhs_ref, f32[16,2048]{1,0:T(8,128)} %reshape_reshape_transpose_reshape.7.coef_ref), custom_call_target="tpu_custom_call" | custom-call | tf_op jit(solution)/shard_map/pallas_call | solution.py:289
  115.6 0.8 dynamic-slice_reduce_fusion
  116.4 0.7 reshape.348
  (90 shorter events, 0.7 us)
Async XLA Ops:
  0.6 15.9 %copy-start = (f32[8,64,256]{2,1,0:T(8,128)S(1)}, f32[8,64,256]{2,1,0:T(8,128)}, u32[]{:S(2)}) copy-start(f32[8,64,256]{2,1,0:T(8,128)} %param.4) | copy-start | bytes 1572868
  0.6 15.0 %copy-start.1 = (f32[8,64,256]{2,1,0:T(8,128)S(1)}, f32[8,64,256]{2,1,0:T(8,128)}, u32[]{:S(2)}) copy-start(f32[8,64,256]{2,1,0:T(8,128)} %param.5) | copy-start | bytes 1572868
  2.4 15.7 %collective-permute-start.7 = (f32[8,7,256]{2,1,0:T(8,128)S(1)}, f32[8,7,256]{2,1,0:T(8,128)S(1)}, u32[]{:S(2)}, u32[]{:S(2)}) collective-permute-start(f32[8,7,256]{2,1,0:T(8,128)S(1)} %pad_maximum_fusion.21), channel_id=1, source_target_pairs={{9,0},{10,1},{11,2},{12,3},{13,4},{14,5},{15,6},{17,8},{18,9},{19,... | collective-permute-start | bytes 172040 | tf_op jit(solution)/shard_map/ppermute | solution.py:87
  3.7 17.5 %collective-permute-start.2 = (f32[8,7,256]{2,1,0:T(8,128)S(1)}, f32[8,7,256]{2,1,0:T(8,128)S(1)}, u32[]{:S(2)}, u32[]{:S(2)}) collective-permute-start(f32[8,7,256]{2,1,0:T(8,128)S(1)} %pad_maximum_fusion.19), channel_id=1, source_target_pairs={{1,8},{2,9},{3,10},{4,11},{5,12},{6,13},{7,14},{9,16},{10,17},{11,... | collective-permute-start | bytes 172040 | tf_op jit(solution)/shard_map/ppermute | solution.py:87
  4.4 18.1 %collective-permute-start.5 = (f32[8,7,256]{2,1,0:T(8,128)S(1)}, f32[8,7,256]{2,1,0:T(8,128)S(1)}, u32[]{:S(2)}, u32[]{:S(2)}) collective-permute-start(f32[8,7,256]{2,1,0:T(8,128)S(1)} %pad_maximum_fusion.20), channel_id=1, source_target_pairs={{8,1},{9,2},{10,3},{11,4},{12,5},{13,6},{14,7},{16,9},{17,10},{18,... | collective-permute-start | bytes 172040 | tf_op jit(solution)/shard_map/ppermute | solution.py:87
  5.1 12.8 %copy-start.2 = (f32[8,64,256]{2,1,0:T(8,128)S(1)}, f32[8,64,256]{2,1,0:T(8,128)}, u32[]{:S(2)}) copy-start(f32[8,64,256]{2,1,0:T(8,128)} %param.3) | copy-start | bytes 1572868
  5.1 22.1 %collective-permute-start = (f32[8,7,256]{2,1,0:T(8,128)S(1)}, f32[8,7,256]{2,1,0:T(8,128)S(1)}, u32[]{:S(2)}, u32[]{:S(2)}) collective-permute-start(f32[8,7,256]{2,1,0:T(8,128)S(1)} %pad_maximum_fusion.18), channel_id=1, source_target_pairs={{0,9},{1,10},{2,11},{3,12},{4,13},{5,14},{6,15},{8,17},{9,18},{10,... | collective-permute-start | bytes 172040 | tf_op jit(solution)/shard_map/ppermute | solution.py:87
  16.6 10.6 %collective-permute-start.4 = (f32[30,7,256]{2,1,0:T(8,128)S(1)}, f32[30,7,256]{2,1,0:T(8,128)S(1)}, u32[]{:S(2)}, u32[]{:S(2)}) collective-permute-start(f32[30,7,256]{2,1,0:T(8,128)S(1)} %constant_dynamic-update-slice_fusion.2), channel_id=1, source_target_pairs={{1,0},{2,1},{3,2},{4,3},{5,4},{6,5},{7,6},{9,8},{10,9},{11,10},{12... | collective-permute-start | bytes 645128 | tf_op jit(solution)/shard_map/ppermute | solution.py:87
  18.1 19.0 %copy-start.3 = (f32[8,7,256]{2,1,0:T(8,128)}, f32[8,7,256]{2,1,0:T(8,128)S(1)}, u32[]{:S(2)}) copy-start(f32[8,7,256]{2,1,0:T(8,128)S(1)} %collective-permute-done.7) | copy-start | bytes 172036
  18.1 9.1 %collective-permute-start.3 = (f32[30,7,256]{2,1,0:T(8,128)S(1)}, f32[30,7,256]{2,1,0:T(8,128)S(1)}, u32[]{:S(2)}, u32[]{:S(2)}) collective-permute-start(f32[30,7,256]{2,1,0:T(8,128)S(1)} %constant_dynamic-update-slice_fusion), channel_id=1, source_target_pairs={{0,1},{1,2},{2,3},{3,4},{4,5},{5,6},{6,7},{8,9},{9,10},{10,11},{11... | collective-permute-start | bytes 645128 | tf_op jit(solution)/shard_map/ppermute | solution.py:87
  21.2 15.9 %copy-start.4 = (f32[8,7,256]{2,1,0:T(8,128)}, f32[8,7,256]{2,1,0:T(8,128)S(1)}, u32[]{:S(2)}) copy-start(f32[8,7,256]{2,1,0:T(8,128)S(1)} %collective-permute-done.2) | copy-start | bytes 172036
  21.2 15.8 %collective-permute-start.6 = (f32[8,64,256]{2,1,0:T(8,128)S(1)}, f32[8,64,256]{2,1,0:T(8,128)S(1)}, u32[]{:S(2)}, u32[]{:S(2)}) collective-permute-start(f32[8,64,256]{2,1,0:T(8,128)S(1)} %pad_maximum_fusion.3), channel_id=1, source_target_pairs={{8,0},{16,8},{24,16},{32,24},{40,32},{48,40},{56,48},{64,56},{72,6... | collective-permute-start | bytes 1572872 | tf_op jit(solution)/shard_map/ppermute | solution.py:87
  22.6 14.6 %copy-start.5 = (f32[8,7,256]{2,1,0:T(8,128)}, f32[8,7,256]{2,1,0:T(8,128)S(1)}, u32[]{:S(2)}) copy-start(f32[8,7,256]{2,1,0:T(8,128)S(1)} %collective-permute-done.5) | copy-start | bytes 172036
  22.6 16.3 %collective-permute-start.1 = (f32[8,64,256]{2,1,0:T(8,128)S(1)}, f32[8,64,256]{2,1,0:T(8,128)S(1)}, u32[]{:S(2)}, u32[]{:S(2)}) collective-permute-start(f32[8,64,256]{2,1,0:T(8,128)S(1)} %pad_maximum_fusion.2), channel_id=1, source_target_pairs={{0,8},{8,16},{16,24},{24,32},{32,40},{40,48},{48,56},{56,64},{64,7... | collective-permute-start | bytes 1572872 | tf_op jit(solution)/shard_map/ppermute | solution.py:87
  27.2 11.7 %copy-start.6 = (f32[8,7,256]{2,1,0:T(8,128)}, f32[8,7,256]{2,1,0:T(8,128)S(1)}, u32[]{:S(2)}) copy-start(f32[8,7,256]{2,1,0:T(8,128)S(1)} %collective-permute-done) | copy-start | bytes 172036
  39.0 1.3 %slice-start = ((f32[8,7,256]{2,1,0:T(8,128)}), f32[2,7,256]{2,1,0:T(8,128)S(1)}, s32[]{:S(2)}) async-start(f32[8,7,256]{2,1,0:T(8,128)} %copy-done.3), calls=%async_computation.1 | async-start | bytes 32768 | tf_op jit(solution)/shard_map/slice | solution.py:91
  39.0 1.3 %slice-start.1 = ((f32[8,7,256]{2,1,0:T(8,128)}), f32[2,7,256]{2,1,0:T(8,128)S(1)}, s32[]{:S(2)}) async-start(f32[8,7,256]{2,1,0:T(8,128)} %copy-done.4), calls=%async_computation.2 | async-start | bytes 32768 | tf_op jit(solution)/shard_map/slice | solution.py:91
  39.0 1.3 %slice-start.2 = ((f32[8,7,256]{2,1,0:T(8,128)}), f32[2,7,256]{2,1,0:T(8,128)S(1)}, s32[]{:S(2)}) async-start(f32[8,7,256]{2,1,0:T(8,128)} %copy-done.5), calls=%async_computation.3 | async-start | bytes 32768 | tf_op jit(solution)/shard_map/slice | solution.py:91
  39.1 1.3 %slice-start.3 = ((f32[8,7,256]{2,1,0:T(8,128)}), f32[2,7,256]{2,1,0:T(8,128)S(1)}, s32[]{:S(2)}) async-start(f32[8,7,256]{2,1,0:T(8,128)} %copy-done.6), calls=%async_computation.4 | async-start | bytes 32768 | tf_op jit(solution)/shard_map/slice | solution.py:91
  45.1 9.3 %collective-permute-start.8 = (f32[7,38,128]{2,1,0:T(8,128)S(1)}, f32[7,38,128]{2,1,0:T(8,128)S(1)}, u32[]{:S(2)}, u32[]{:S(2)}) collective-permute-start(f32[7,38,128]{2,1,0:T(8,128)S(1)} %get-tuple-element.94), channel_id=1, source_target_pairs={{0,8},{8,16},{16,24},{24,32},{32,40},{40,48},{48,56},{56,64},{64,7... | collective-permute-start | bytes 408584 | tf_op jit(solution)/shard_map/ppermute | solution.py:58
  50.4 10.7 %collective-permute-start.9 = (f32[7,38,128]{2,1,0:T(8,128)S(1)}, f32[7,38,128]{2,1,0:T(8,128)S(1)}, u32[]{:S(2)}, u32[]{:S(2)}) collective-permute-start(f32[7,38,128]{2,1,0:T(8,128)S(1)} %get-tuple-element.95), channel_id=1, source_target_pairs={{8,0},{16,8},{24,16},{32,24},{40,32},{48,40},{56,48},{64,56},{72,6... | collective-permute-start | bytes 408584 | tf_op jit(solution)/shard_map/ppermute | solution.py:58
  62.7 2.7 %collective-permute-start.10 = (f32[2,3,64]{2,1,0:T(4,128)S(1)}, f32[2,3,64]{2,1,0:T(4,128)S(1)}, u32[]{:S(2)}, u32[]{:S(2)}) collective-permute-start(f32[2,3,64]{2,1,0:T(4,128)S(1)} %get-tuple-element.96), channel_id=1, source_target_pairs={{0,1},{1,2},{2,3},{3,4},{4,5},{5,6},{6,7},{8,9},{9,10},{10,11},{11... | collective-permute-start | bytes 4616 | tf_op jit(solution)/shard_map/ppermute | solution.py:58
  64.1 4.7 %collective-permute-start.11 = (f32[2,3,64]{2,1,0:T(4,128)S(1)}, f32[2,3,64]{2,1,0:T(4,128)S(1)}, u32[]{:S(2)}, u32[]{:S(2)}) collective-permute-start(f32[2,3,64]{2,1,0:T(4,128)S(1)} %get-tuple-element.97), channel_id=1, source_target_pairs={{1,0},{2,1},{3,2},{4,3},{5,4},{6,5},{7,6},{9,8},{10,9},{11,10},{12... | collective-permute-start | bytes 4616 | tf_op jit(solution)/shard_map/ppermute | solution.py:58
  68.7 7.3 %collective-permute-start.12 = (f32[3,22,64]{2,1,0:T(8,128)S(1)}, f32[3,22,64]{2,1,0:T(8,128)S(1)}, u32[]{:S(2)}, u32[]{:S(2)}) collective-permute-start(f32[3,22,64]{2,1,0:T(8,128)S(1)} %get-tuple-element.92), channel_id=1, source_target_pairs={{0,8},{8,16},{16,24},{24,32},{32,40},{40,48},{48,56},{56,64},{64,7... | collective-permute-start | bytes 50696 | tf_op jit(solution)/shard_map/ppermute | solution.py:58
  74.6 8.4 %collective-permute-start.13 = (f32[3,22,64]{2,1,0:T(8,128)S(1)}, f32[3,22,64]{2,1,0:T(8,128)S(1)}, u32[]{:S(2)}, u32[]{:S(2)}) collective-permute-start(f32[3,22,64]{2,1,0:T(8,128)S(1)} %get-tuple-element.93), channel_id=1, source_target_pairs={{8,0},{16,8},{24,16},{32,24},{40,32},{48,40},{56,48},{64,56},{72,6... | collective-permute-start | bytes 50696 | tf_op jit(solution)/shard_map/ppermute | solution.py:58
  85.2 25.0 %all-to-all-start = ((f32[128,1,512]{2,1,0:T(1,128)}), f32[128,1,512]{2,1,0:T(1,128)S(1)}, u32[]{:S(2)}, u32[]{:S(2)}) async-start(f32[128,1,512]{2,1,0:T(1,128)} %broadcast_in_dim.34), calls=%async_computation | async-start | bytes 524288 | tf_op jit(solution)/shard_map/all_to_all | solution.py:240
